TPU v7x, 256 devices: a whole 4x4x8 slice. The times are simulated.
256 devices in a mesh: row: 32 (over x, z), col: 8 (over y, core).
Axes of the slice: x: 4, y: 4, z: 8, core: 2. Of those that a mesh axis runs over, the one named last changes fastest.
Arguments:
- points: float32 [16384, 256], P('row'), may hold values from -6 to 6
- nugget: float32 [16384], P('row'), may hold values from 0.5 to 2
- weights: float32 [256], replicated, may hold values from 0.0005 to 0.005
- band_start: int32 [32], replicated, may hold values from 0 to 30, as said below
Outputs:
- factored: float32 [32, 4, 8, 512, 512], P('row', None, 'col')
Inputs may be any that keep to these rules, and one draw needn't show every extreme that they name: band_start[i] <= i - 1 for every i >= 1, band_start[0] = 0; band_start[17] = 0; the last tile row has band_start = 30.
All inputs are finite; a program needn't handle non-finite values.
Results may differ from a plain program's by a relative error of at most 0.0003.
Values sent between devices are 32-bit elements; how exact they have to be, the bound alone decides.
No kernel may reach another device: no remote copies, remote signals or barrier semaphores. Data moves between devices by JAX's collectives and lax.ppermute only.
A program may use at most 128 MiB of HBM per device.

v0:
```python
import jax
import jax.numpy as jnp
from jax import lax
from jax.sharding import PartitionSpec as P


def broadcast(value, axis, source):
    kept = jnp.where(lax.axis_index(axis) == source, value, 0).astype(value.dtype)
    return lax.psum(kept, axis)


def kernel_tile(xrow, xcol, weights):
    weighted = xrow * weights
    sq_row = jnp.sum(weighted * xrow, axis=1)
    sq_col = jnp.sum(xcol * xcol * weights, axis=1)
    cross = jnp.dot(
        weighted, xcol.T, precision=lax.Precision.HIGHEST, preferred_element_type=jnp.float32
    )
    dist_sq = jnp.maximum(sq_row[:, None] + sq_col[None, :] - 2.0 * cross, 0.0)
    dist = jnp.sqrt(3.0 * dist_sq)
    return (1.0 + dist) * jnp.exp(-dist)


def factor_panel(local, p, n_col, my_row):
    owner_col = p % n_col
    diag_tile = broadcast(local, "row", p)
    lpp = jnp.linalg.cholesky(diag_tile)
    solved = jax.scipy.linalg.solve_triangular(lpp, local.T, lower=True).T
    panel = broadcast(solved, "col", owner_col)
    panel = jnp.where(my_row > p, panel, jnp.where(my_row == p, lpp, jnp.float32(0.0)))
    return panel


def column_factors(panel, my_col, n_col, blocks):
    width = panel.shape[1]
    slab = panel.shape[0] // (n_col * blocks)
    mixed = lax.all_to_all(panel, "row", split_axis=0, concat_axis=0, tiled=True)
    picked = lax.dynamic_slice_in_dim(mixed.reshape(blocks, n_col, slab, width), my_col, 1, 1)
    picked = picked.reshape(blocks, slab, width)
    whole = lax.all_gather(picked, "row", axis=1, tiled=True)
    return [whole[k] for k in range(blocks)]


def apply_panel(tiles, panel, col_tiles, p, my_row, my_col, n_col):
    result = []
    for k in range(len(tiles)):
        column = my_col + n_col * k
        prod = jnp.dot(
            panel,
            col_tiles[k].T,
            precision=lax.Precision.HIGHEST,
            preferred_element_type=jnp.float32,
        )
        live = (column > p) & (column <= my_row)
        block = tiles[k] - jnp.where(live, prod, jnp.float32(0.0))
        result.append(jnp.where(column == p, panel, block))
    return result


def body(points, nugget, weights, band_start):
    n_row = lax.axis_size("row")
    n_col = lax.axis_size("col")
    blocks = n_row // n_col
    my_row = lax.axis_index("row")
    my_col = lax.axis_index("col")
    diag_nugget = jnp.diag(nugget)
    tiles = []
    for k in range(blocks):
        column = my_col + n_col * k
        xcol = broadcast(points, "row", column)
        block = kernel_tile(points, xcol, weights)
        keep = (column >= band_start[my_row]) & (column <= my_row)
        block = jnp.where(keep, block, jnp.float32(0.0))
        tiles.append(block + jnp.where(column == my_row, diag_nugget, jnp.float32(0.0)))
    for p in range(2):
        panel = factor_panel(tiles[p // n_col], p, n_col, my_row)
        col_tiles = column_factors(panel, my_col, n_col, blocks)
        tiles = apply_panel(tiles, panel, col_tiles, p, my_row, my_col, n_col)
    stacked_tiles = jnp.stack(tiles)
    return stacked_tiles.reshape(1, blocks, 1, points.shape[0], points.shape[0])


def solution(mesh):
    placed = (P("row", None), P("row"), P(), P())
    return jax.shard_map(
        body,
        mesh=mesh,
        in_specs=placed,
        out_specs=P("row", None, "col", None, None),
        check_vma=False,
    )
```

profile of v0, /device:TPU:8, one launch (start us, length us, event | category | flops | bytes accessed | tf_op | source)
XLA Modules:
  0.0 1198.2 jit_solution(10139373326444151370)
XLA Ops:
  10.4 158.8 %all-reduce.16.cloned.1.call-done = (f32[512,256]{1,0:T(8,128)}, f32[512,256]{1,0:T(8,128)}, f32[512,256]{1,0:T(8,128)}, f32[512,256]{1,0:T(8,128)}) async-done(((f32[512,256]{1,0:T(8,128)}, f32[512,256]{1,0:T(8,128)}, f32[512,256]{1,0:T(8,128)}, f32[512,256]{1,0:T(8,128)}), (f32[512,256]{1,0:T(8,128)}, f32[512,256]{1,0:T(8,128)}, f32[512,256]{1,0:T(8,128)}, ...) | async-done | bytes 2097168 | tf_op jit(solution)/shard_map/psum | solution.py:9
  178.3 147.6 %all-reduce.8.cloned.1.call-done = f32[512,512]{0,1:T(8,128)} async-done(((f32[512,512]{0,1:T(8,128)}), f32[512,512]{0,1:T(8,128)}) %all-reduce.8.cloned.1.call-update) | async-done | bytes 1048592 | tf_op jit(solution)/shard_map/psum | solution.py:9
  329.9 11.7 cholesky.286
  341.7 9.8 custom-call.27
  354.2 11.7 cholesky.305
  366.1 10.0 custom-call.28
  378.1 11.7 cholesky.326
  389.9 9.8 custom-call.29
  401.4 12.1 %cholesky.343 = f32[128,128]{1,0:T(8,128)S(1)} custom-call(f32[128,128]{1,0:T(8,128)S(1)} %convolution_subtract_fusion.11), custom_call_target="Cholesky" | custom-call | tf_op jit(solution)/shard_map/jit(cholesky)/cholesky | solution.py:27
  419.3 12.3 %while.4 = (s32[]{:T(128)}, f32[512,512]{0,1:T(8,128)}, s32[4,2]{0,1:T(2,128)S(1)}, f32[4,128,128]{2,1,0:T(8,128)S(1)}, s32[]{:T(128)}) while((s32[]{:T(128)}, f32[512,512]{0,1:T(8,128)}, s32[4,2]{0,1:T(2,128)S(1)}, f32[4,128,128]{2,1,0:T(8,128)S(1)}, s32[]{:T(128)}) %tuple.57), condition=%wide.while_cond, body=%wide.while_body.sunk | while | flops 2 | bytes 393329 | solution.py:28
  431.6 39.3 %custom-call.30 = f32[4,128,128]{1,2,0:T(8,128)S(1)} custom-call(f32[4,128,128]{2,1,0:T(8,128)S(1)} %get-tuple-element.21), custom_call_target="InvertDiagBlocksLowerTriangular" | custom-call | tf_op jit(solution)/shard_map/jit(_solve_triangular)/triangular_solve | solution.py:28
  486.3 62.9 %all-reduce.10.cloned.1.call-done = f32[512,512]{1,0:T(8,128)} async-done(((f32[512,512]{1,0:T(8,128)}), f32[512,512]{1,0:T(8,128)}) %all-reduce.10.cloned.1.call-update) | async-done | bytes 1048592 | tf_op jit(solution)/shard_map/psum | solution.py:9
  555.4 11.0 all-to-all-start
  566.5 26.7 %all-to-all-done = f32[32,16,512]{2,1,0:T(8,128)S(1)} async-done(((f32[32,16,512]{2,1,0:T(8,128)}), f32[32,16,512]{2,1,0:T(8,128)S(1)}, u32[]{:S(2)}, u32[]{:S(2)}) %all-to-all-start) | async-done | bytes 1048608 | tf_op jit(solution)/shard_map/all_to_all | solution.py:37
  593.9 81.1 %all-gather.5.cloned.1.call-done = f32[4,1,512,512]{3,2,1,0:T(8,128)} async-done(((f32[4,1,16,512]{3,2,1,0:T(8,128)}), f32[4,1,512,512]{3,2,1,0:T(8,128)}) %all-gather.5.cloned.1.call-update) | async-done | bytes 4194320 | tf_op jit(solution)/shard_map/all_gather | solution.py:40
  675.0 5.4 broadcast_select_fusion
  680.7 147.2 %all-reduce.12.cloned.1.call-done = f32[512,512]{0,1:T(8,128)} async-done(((f32[512,512]{0,1:T(8,128)}), f32[512,512]{0,1:T(8,128)}) %all-reduce.12.cloned.1.call-update) | async-done | bytes 1048592 | tf_op jit(solution)/shard_map/psum | solution.py:9
  831.9 11.7 cholesky.358
  843.7 9.8 custom-call.31
  856.2 11.7 cholesky.377
  868.1 10.0 custom-call.32
  880.1 11.7 cholesky.398
  891.9 9.8 custom-call.33
  903.4 12.1 %cholesky.415 = f32[128,128]{1,0:T(8,128)S(1)} custom-call(f32[128,128]{1,0:T(8,128)S(1)} %convolution_subtract_fusion.10), custom_call_target="Cholesky" | custom-call | tf_op jit(solution)/shard_map/jit(cholesky)/cholesky | solution.py:27
  921.9 12.3 %while.5 = (s32[]{:T(128)}, f32[512,512]{0,1:T(8,128)}, s32[4,2]{0,1:T(2,128)S(1)}, f32[4,128,128]{2,1,0:T(8,128)S(1)}, s32[]{:T(128)}) while((s32[]{:T(128)}, f32[512,512]{0,1:T(8,128)}, s32[4,2]{0,1:T(2,128)S(1)}, f32[4,128,128]{2,1,0:T(8,128)S(1)}, s32[]{:T(128)}) %tuple.78), condition=%wide.while_cond.clone, body=%wide.while_body.clone.sunk | while | flops 2 | bytes 393329 | solution.py:28
  934.2 39.3 %custom-call.34 = f32[4,128,128]{1,2,0:T(8,128)S(1)} custom-call(f32[4,128,128]{2,1,0:T(8,128)S(1)} %get-tuple-element.22), custom_call_target="InvertDiagBlocksLowerTriangular" | custom-call | tf_op jit(solution)/shard_map/jit(_solve_triangular)/triangular_solve | solution.py:28
  986.2 62.8 %all-reduce.14.cloned.1.call-done = f32[512,512]{1,0:T(8,128)} async-done(((f32[512,512]{1,0:T(8,128)}), f32[512,512]{1,0:T(8,128)}) %all-reduce.14.cloned.1.call-update) | async-done | bytes 1048592 | tf_op jit(solution)/shard_map/psum | solution.py:9
  1053.1 38.0 %all_to_all.18 = f32[32,16,512]{2,1,0:T(8,128)S(1)} all-to-all(f32[32,16,512]{2,1,0:T(8,128)} %bitcast.160), channel_id=1, replica_groups=mesh['row'=32,'col'=8] {'row'}, dimensions={0} | all-to-all | bytes 2097152 | tf_op jit(solution)/shard_map/all_to_all | solution.py:37
  1109.6 63.2 %all-gather.7.cloned.1.call-done = f32[4,1,512,512]{3,2,1,0:T(8,128)} async-done(((f32[4,1,16,512]{3,2,1,0:T(8,128)}), f32[4,1,512,512]{3,2,1,0:T(8,128)}) %all-gather.7.cloned.1.call-update) | async-done | bytes 4194320 | tf_op jit(solution)/shard_map/all_gather | solution.py:40
  1172.8 3.2 fusion.29
  1176.1 3.4 fusion.19
  1185.9 5.2 copy.94
  (196 shorter events, 127.0 us)
Async XLA Ops:
  6.5 162.6 %copy-start = (f32[512,256]{1,0:T(8,128)S(1)}, f32[512,256]{1,0:T(8,128)}, u32[]{:S(2)}) copy-start(f32[512,256]{1,0:T(8,128)} %param.7) | copy-start | bytes 1572868
  6.5 2.6 copy-start.16
  6.5 162.6 %copy-start.13 = (f32[256]{0:T(256)S(1)}, f32[256]{0:T(256)}, u32[]{:S(2)}) copy-start(f32[256]{0:T(256)} %param.9) | copy-start | bytes 3076
  6.5 162.6 %all-reduce.16.cloned.1.call-start = ((), (), s32[]{:S(2)}) async-start(), calls=%async_computation.8 | async-start | bytes 4194304 | tf_op jit(solution)/shard_map/psum | solution.py:9
  9.0 166.8 %copy-start.14 = (f32[512]{0:T(512)S(1)}, f32[512]{0:T(512)}, u32[]{:S(2)}) copy-start(f32[512]{0:T(512)} %param.8) | copy-start | bytes 6148
  9.1 316.8 %all-reduce.8.cloned.1.call-start = ((), (), s32[]{:S(2)}) async-start(), calls=%async_computation.2 | async-start | bytes 2097152 | tf_op jit(solution)/shard_map/psum | solution.py:9
  178.1 371.0 %all-reduce.10.cloned.1.call-start = ((), (), s32[]{:S(2)}) async-start(), calls=%async_computation.3 | async-start | bytes 2097152 | tf_op jit(solution)/shard_map/psum | solution.py:9
  328.9 1.0 copy-start.6
  471.0 5.2 copy-start.11
  555.4 37.8 %all-to-all-start = ((f32[32,16,512]{2,1,0:T(8,128)}), f32[32,16,512]{2,1,0:T(8,128)S(1)}, u32[]{:S(2)}, u32[]{:S(2)}) async-start(f32[32,16,512]{2,1,0:T(8,128)} %bitcast.14), calls=%async_computation | async-start | bytes 2097152 | tf_op jit(solution)/shard_map/all_to_all | solution.py:37
  566.4 108.6 %all-gather.5.cloned.1.call-start = ((), (), s32[]{:S(2)}) async-start(), calls=%async_computation.6 | async-start | bytes 4325376 | tf_op jit(solution)/shard_map/all_gather | solution.py:40
  593.9 234.0 %all-reduce.12.cloned.1.call-start = ((), (), s32[]{:S(2)}) async-start(), calls=%async_computation.4 | async-start | bytes 2097152 | tf_op jit(solution)/shard_map/psum | solution.py:9
  680.4 299.6 %copy-start.2 = (f32[512,512]{0,1:T(8,128)}, f32[512,512]{0,1:T(8,128)S(1)}, u32[]{:S(2)}) copy-start(f32[512,512]{0,1:T(8,128)S(1)} %get-tuple-element.89) | copy-start | bytes 3145732
  680.5 368.5 %all-reduce.14.cloned.1.call-start = ((), (), s32[]{:S(2)}) async-start(), calls=%async_computation.5 | async-start | bytes 2097152 | tf_op jit(solution)/shard_map/psum | solution.py:9
  830.9 1.0 copy-start.7
  973.5 3.8 copy-start.12
  986.1 186.7 %all-gather.7.cloned.1.call-start = ((), (), s32[]{:S(2)}) async-start(), calls=%async_computation.7 | async-start | bytes 4325376 | tf_op jit(solution)/shard_map/all_gather | solution.py:40
  1051.7 47.1 %copy-start.8 = (f32[512,256]{1,0:T(8,128)S(1)}, f32[512,256]{1,0:T(8,128)}, u32[]{:S(2)}) copy-start(f32[512,256]{1,0:T(8,128)} %get-tuple-element.63) | copy-start | bytes 1572868
  1053.1 47.2 %copy-start.4 = (f32[512,512]{0,1:T(8,128)S(1)}, f32[512,512]{0,1:T(8,128)}, u32[]{:S(2)}) copy-start(f32[512,512]{0,1:T(8,128)} %select_select_fusion.5) | copy-start | bytes 3145732
  1093.6 6.7 copy-start.15
  1096.2 7.1 copy-start.5
  1103.3 69.5 %copy-start.3 = (f32[512,512]{0,1:T(8,128)S(1)}, f32[512,512]{0,1:T(8,128)}, u32[]{:S(2)}) copy-start(f32[512,512]{0,1:T(8,128)} %copy-done.2) | copy-start | bytes 3145732
  1172.8 3.3 copy-start.1
  1172.8 6.7 copy-start.9
  1176.1 5.5 copy-start.10
Sparse Core Ops, SparseCore 0:
  11.2 157.8 all-reduce.15
  178.2 147.6 all-reduce.7
  486.4 62.7 all-reduce.9
  594.0 80.9 all-gather.4
  680.6 147.2 all-reduce.11
  986.3 62.7 all-reduce.13
  1091.8 80.9 all-gather.6
where the time goes:
time: 1200 us
  waiting for transfers between devices  750 us (62%)
  other arithmetic  257 us (21%)
  matrix products  67 us (6%)
  local copies, waits for them, and re-layouts  52.1 us (4%)
  blocking collectives  38 us (3%)
  between operations  22.1 us (2%)
    psum x5, waiting for transfers between devices, broadcast(): return lax.psum(kept, axis)  579 us
    another operation x29, other arithmetic, factor_panel(): lpp = jnp.linalg.cholesky(diag_tile)  159 us
    all_gather x2, waiting for transfers between devices, column_factors(): whole = lax.all_gather(picked, 'row', axis=1, tiled=True)  144 us
    another operation x5, other arithmetic, factor_panel(): solved = jax.scipy.linalg.solve_triangular(lpp, local.T, lower=True).T  80.8 us
    all_to_all x1, blocking collectives, column_factors(): lax.all_to_all(panel, 'row', split_axis=0, concat_axis=0, tiled=True)  38 us
    another operation x49, local copies, waits for them, and re-layouts, factor_panel(): solved = jax.scipy.linalg.solve_triangular(lpp, local.T, lower=True).T  28 us
    all_to_all x1, waiting for transfers between devices, column_factors(): lax.all_to_all(panel, 'row', split_axis=0, concat_axis=0, tiled=True)  26.7 us
    dot_general x8, matrix products, apply_panel(): jnp.dot(panel, col_tiles[k].T, precision=lax.Precision.HIGHEST, preferred...  25.5 us
  transfers between devices with their start and end apart: 8, of which 8 were waited for; matrix products, arithmetic and copies ran while one was open for 1% of the time, Pallas kernels for 0%

commit v1 on v0

v1 whole, which is shorter than its diff:
```python
import jax
import jax.numpy as jnp
from jax import lax
from jax.sharding import PartitionSpec as P

HI = lax.Precision.HIGHEST


def mm(a, b):
    return lax.dot_general(
        a, b, (((1,), (1,)), ((), ())), precision=HI, preferred_element_type=jnp.float32
    )


def kernel_tile(xrow, xcol, weights):
    weighted = xrow * weights
    sq_row = jnp.sum(weighted * xrow, axis=1)
    sq_col = jnp.sum(xcol * xcol * weights, axis=1)
    cross = mm(weighted, xcol)
    dist_sq = jnp.maximum(sq_row[:, None] + sq_col[None, :] - 2.0 * cross, 0.0)
    dist = jnp.sqrt(3.0 * dist_sq)
    return (1.0 + dist) * jnp.exp(-dist)


def chol_inv(a):
    low = jnp.linalg.cholesky(a)
    eye = jnp.eye(a.shape[0], dtype=a.dtype)
    inv = jax.scipy.linalg.solve_triangular(low, eye, lower=True)
    return low, inv


def body(points, nugget, weights, band_start):
    n_row = lax.axis_size("row")
    n_col = lax.axis_size("col")
    blocks = n_row // n_col
    tile = points.shape[0]
    piece = tile // n_row
    my_row = lax.axis_index("row")
    my_col = lax.axis_index("col")

    chunks = points.reshape(n_row, piece, points.shape[1])
    recv = lax.all_to_all(chunks, "row", 0, 0, tiled=True)
    mine = lax.dynamic_slice_in_dim(
        recv.reshape(blocks, n_col, piece, points.shape[1]), my_col, 1, axis=1
    )[:, 0]
    sel = jnp.concatenate([recv[:2], mine], axis=0)
    tiles_x = lax.all_gather(sel, "row", axis=1, tiled=True)
    nug = lax.all_gather(nugget, "row", tiled=True)
    x0, x1 = tiles_x[0], tiles_x[1]
    xcols = tiles_x[2:]
    n0, n1 = nug[:tile], nug[tile : 2 * tile]

    cols = my_col + n_col * jnp.arange(blocks, dtype=jnp.int32)
    rows = jnp.concatenate([my_row[None], cols])
    xr_all = jnp.concatenate([points[None], xcols], axis=0).reshape(-1, points.shape[1])
    nr = len(rows)
    eye = jnp.eye(tile, dtype=jnp.float32)

    x01 = jnp.concatenate([x0, x1], axis=0)
    k01 = kernel_tile(x01, x01, weights)
    a00 = k01[:tile, :tile] + eye * n0[None, :]
    a10 = k01[tile:, :tile]
    a11 = k01[tile:, tile:] + eye * n1[None, :]

    kr = kernel_tile(xr_all, x01, weights).reshape(nr, tile, 2, tile)
    bs = band_start[rows]
    keep0 = (bs <= 0)[:, None, None]
    keep1 = ((bs <= 1) & (rows >= 1))[:, None, None]
    ar0 = jnp.where(keep0, kr[:, :, 0], 0.0)
    ar0 = ar0 + jnp.where((rows == 0)[:, None, None], eye * n0[None, :], 0.0)
    ar1 = jnp.where(keep1, kr[:, :, 1], 0.0)
    ar1 = ar1 + jnp.where((rows == 1)[:, None, None], eye * n1[None, :], 0.0)

    l00, m0 = chol_inv(a00)
    stack0 = jnp.concatenate([a10, ar0.reshape(-1, tile)], axis=0)
    sol0 = mm(stack0, m0)
    l01 = sol0[:tile]
    lr0 = sol0[tile:].reshape(nr, tile, tile)
    lr0 = jnp.where((rows == 0)[:, None, None], l00[None], lr0)

    s11 = a11 - mm(l01, l01)
    upd1 = mm(lr0.reshape(-1, tile), l01).reshape(nr, tile, tile)
    ar1 = ar1 - jnp.where((rows >= 1)[:, None, None], upd1, 0.0)
    l11, m1 = chol_inv(s11)
    lr1 = mm(ar1.reshape(-1, tile), m1).reshape(nr, tile, tile)
    lr1 = jnp.where((rows > 1)[:, None, None], lr1, jnp.where((rows == 1)[:, None, None], l11[None], 0.0))

    kout = kernel_tile(points, xcols.reshape(-1, points.shape[1]), weights)
    kout = kout.reshape(tile, blocks, tile).transpose(1, 0, 2)
    bsr = band_start[my_row]
    keep = ((cols >= bsr) & (cols <= my_row))[:, None, None]
    aout = jnp.where(keep, kout, 0.0)
    aout = aout + jnp.where((cols == my_row)[:, None, None], eye * nugget[None, :], 0.0)
    left = jnp.concatenate([lr0[0], lr1[0]], axis=1)
    right = jnp.concatenate([lr0[1:], lr1[1:]], axis=2).reshape(-1, 2 * tile)
    prod = mm(left, right).reshape(tile, blocks, tile).transpose(1, 0, 2)
    live = ((cols > 1) & (cols <= my_row))[:, None, None]
    res = aout - jnp.where(live, prod, 0.0)
    res = jnp.where((cols == 0)[:, None, None], lr0[0][None], res)
    res = jnp.where((cols == 1)[:, None, None], lr1[0][None], res)
    return res.reshape(1, blocks, 1, tile, tile)


def solution(mesh):
    placed = (P("row", None), P("row"), P(), P())
    return jax.shard_map(
        body,
        mesh=mesh,
        in_specs=placed,
        out_specs=P("row", None, "col", None, None),
        check_vma=False,
    )
```

time: 1200 us -> 575 us (0.48)
  waiting for transfers between devices: 750 us -> 38.8 us
  matrix products: 67 us -> 108 us
  local copies, waits for them, and re-layouts: 52.1 us -> 79.1 us
    psum x5 -> x0, waiting for transfers between devices: 579 us -> none  [broadcast(): return lax.psum(kept, axis)]
    all_gather x2 -> x1, waiting for transfers between devices: 144 us -> 22.2 us  [body(): tiles_x = lax.all_gather(sel, 'row', axis=1, tiled=True)]
    all_gather x0 -> x1, blocking collectives: none -> 48.4 us  [body(): nug = lax.all_gather(nugget, 'row', tiled=True)]
    dot_general x12 -> x8, matrix products: 35.2 us -> 80.4 us  [mm(): lax.dot_general(a, b, (((1,), (1,)), ((), ())), precision=HI, preferred_e...]
    all_to_all x1 -> x0, blocking collectives: 38 us -> none  [column_factors(): lax.all_to_all(panel, 'row', split_axis=0, concat_axis=0, tiled=True)]
    slice x0 -> x8, local copies, waits for them, and re-layouts: none -> 16.4 us  [the longest x1 13.8 us: body(): ar1 = jnp.where(keep1, kr[:, :, 1], 0.0)]
    unnamed x34 -> x52, local copies, waits for them, and re-layouts: 2 us -> 14.4 us
    another operation x75 -> x35, local copies, waits for them, and re-layouts: 29.3 us -> 23.6 us  [the longest x27 23.4 us: chol_inv(): inv = jax.scipy.linalg.solve_triangular(low, eye, lower=True)]
  transfers between devices with their start and end apart: 8 -> 2, of which waited for: 8 -> 2; matrix products, arithmetic and copies ran while one was open for 1% -> 1% of each run, Pallas kernels for 0% -> 0%
where the time goes in v1:
time: 575 us; the launch traced here: 564 us
  other arithmetic  259 us (45%)
  matrix products  108 us (19%)
  local copies, waits for them, and re-layouts  79.1 us (14%)
  blocking collectives  48.4 us (8%)
  waiting for transfers between devices  38.8 us (7%)
  between operations  19.4 us (3%)
  starting transfers between devices  11.5 us (2%)
    another operation x29, other arithmetic, chol_inv(): low = jnp.linalg.cholesky(a)  159 us
    another operation x5, other arithmetic, chol_inv(): inv = jax.scipy.linalg.solve_triangular(low, eye, lower=True)  81.5 us
    dot_general x8, matrix products, mm(): lax.dot_general(a, b, (((1,), (1,)), ((), ())), precision=HI, preferred_e...  80.4 us
    all_gather x1, blocking collectives, body(): nug = lax.all_gather(nugget, 'row', tiled=True)  48.4 us
    another operation x27, local copies, waits for them, and re-layouts, chol_inv(): inv = jax.scipy.linalg.solve_triangular(low, eye, lower=True)  23.4 us
    all_gather x1, waiting for transfers between devices, body(): tiles_x = lax.all_gather(sel, 'row', axis=1, tiled=True)  22.2 us
    all_to_all x1, waiting for transfers between devices, body(): recv = lax.all_to_all(chunks, 'row', 0, 0, tiled=True)  16.6 us
    another operation x14, matrix products, chol_inv(): inv = jax.scipy.linalg.solve_triangular(low, eye, lower=True)  16.6 us
  transfers between devices with their start and end apart: 2, of which 2 were waited for; matrix products, arithmetic and copies ran while one was open for 1% of the time, Pallas kernels for 0%

profile of v1, /device:TPU:8, one launch (start us, length us, event | category | flops | bytes accessed | tf_op | source)
XLA Modules:
  0.0 564.2 jit_solution(12527684723368307736)
XLA Ops:
  6.5 11.4 %all-to-all-start = ((f32[32,16,256]{2,1,0:T(8,128)}), f32[32,16,256]{2,1,0:T(8,128)S(1)}, u32[]{:S(2)}, u32[]{:S(2)}) async-start(f32[32,16,256]{2,1,0:T(8,128)} %bitcast.199), calls=%async_computation | async-start | bytes 1048576 | tf_op jit(solution)/shard_map/all_to_all | solution.py:42
  18.1 16.6 %all-to-all-done = f32[32,16,256]{2,1,0:T(8,128)S(1)} async-done(((f32[32,16,256]{2,1,0:T(8,128)}), f32[32,16,256]{2,1,0:T(8,128)S(1)}, u32[]{:S(2)}, u32[]{:S(2)}) %all-to-all-start) | async-done | bytes 524320 | tf_op jit(solution)/shard_map/all_to_all | solution.py:42
  37.1 48.4 %all-gather = f32[32,1,512]{2,1,0:T(1,128)S(1)} all-gather(f32[1,1,512]{2,1,0:T(1,128)} %bitcast.205), channel_id=1, replica_groups=mesh['row'=32,'col'=8] {'row'}, dimensions={0}, use_global_device_ids=true | all-gather | bytes 67584 | tf_op jit(solution)/shard_map/all_gather | solution.py:48
  90.2 22.2 %all-gather.3.cloned.1.call-done = f32[6,512,256]{2,1,0:T(8,128)} async-done(((f32[6,16,256]{2,1,0:T(8,128)}), f32[6,512,256]{2,1,0:T(8,128)}) %all-gather.3.cloned.1.call-update) | async-done | bytes 3145744 | tf_op jit(solution)/shard_map/all_gather | solution.py:47
  114.0 5.7 %exponential_multiply_fusion.2 = f32[1024,1024]{0,1:T(8,128)S(1)} fusion(f32[1024]{0:T(1024)S(1)} %get-tuple-element.24, f32[1024]{0:T(1024)S(1)} %get-tuple-element.23, f32[256]{0:T(256)S(1)} %copy-done.21, f32[512,256]{1,0:T(8,128)S(1)} %get-tuple-element.58, f32[512,256]{1,0:T(8,128)S(1)} %get-tuple-element.57), kind=kOutput, calls=%fused_computation.34 | convolution fusion | flops 3230400512 | bytes 5252096 | tf_op jit(solution)/shard_map/dot_general | solution.py:10
  123.9 11.9 %cholesky.286 = f32[128,128]{1,0:T(8,128)S(1)} custom-call(f32[128,128]{1,0:T(8,128)S(1)} %cholesky.426), custom_call_target="Cholesky" | custom-call | tf_op jit(solution)/shard_map/jit(cholesky)/cholesky | solution.py:26
  136.0 9.8 %custom-call.27 = f32[1,128,128]{1,2,0:T(8,128)S(1)} custom-call(f32[1,128,128]{2,1,0:T(8,128)S(1)} %get-tuple-element.84), custom_call_target="InvertDiagBlocksLowerTriangular" | custom-call | tf_op jit(solution)/shard_map/jit(cholesky)/cholesky | solution.py:26
  148.4 11.7 %cholesky.305 = f32[128,128]{1,0:T(8,128)S(1)} custom-call(f32[128,128]{1,0:T(8,128)S(1)} %cholesky.430), custom_call_target="Cholesky" | custom-call | tf_op jit(solution)/shard_map/jit(cholesky)/cholesky | solution.py:26
  160.1 9.8 %custom-call.28 = f32[1,128,128]{1,2,0:T(8,128)S(1)} custom-call(f32[1,128,128]{2,1,0:T(8,128)S(1)} %get-tuple-element.81), custom_call_target="InvertDiagBlocksLowerTriangular" | custom-call | tf_op jit(solution)/shard_map/jit(cholesky)/cholesky | solution.py:26
  171.5 12.1 %cholesky.326 = f32[128,128]{1,0:T(8,128)S(1)} custom-call(f32[128,128]{1,0:T(8,128)S(1)} %cholesky.435), custom_call_target="Cholesky" | custom-call | tf_op jit(solution)/shard_map/jit(cholesky)/cholesky | solution.py:26
  184.3 9.8 %custom-call.29 = f32[1,128,128]{1,2,0:T(8,128)S(1)} custom-call(f32[1,128,128]{2,1,0:T(8,128)S(1)} %get-tuple-element.78), custom_call_target="InvertDiagBlocksLowerTriangular" | custom-call | tf_op jit(solution)/shard_map/jit(cholesky)/cholesky | solution.py:26
  195.6 11.7 %cholesky.343 = f32[128,128]{1,0:T(8,128)S(1)} custom-call(f32[128,128]{1,0:T(8,128)S(1)} %convolution_subtract_fusion.12), custom_call_target="Cholesky" | custom-call | tf_op jit(solution)/shard_map/jit(cholesky)/cholesky | solution.py:26
  212.4 12.1 %while.4 = (s32[]{:T(128)}, f32[512,512]{1,0:T(8,128)}, s32[4,2]{0,1:T(2,128)S(1)}, f32[4,128,128]{2,1,0:T(8,128)S(1)}, s32[]{:T(128)}) while((s32[]{:T(128)}, f32[512,512]{1,0:T(8,128)}, s32[4,2]{0,1:T(2,128)S(1)}, f32[4,128,128]{2,1,0:T(8,128)S(1)}, s32[]{:T(128)}) %tuple.69), condition=%wide.while_cond, body=%wide.while_body.sunk | while | flops 2 | bytes 131181 | solution.py:28
  224.5 39.3 %custom-call.30 = f32[4,128,128]{1,2,0:T(8,128)S(1)} custom-call(f32[4,128,128]{2,1,0:T(8,128)S(1)} %get-tuple-element.21), custom_call_target="InvertDiagBlocksLowerTriangular" | custom-call | tf_op jit(solution)/shard_map/jit(_solve_triangular)/triangular_solve | solution.py:28
  279.6 17.8 %exponential_multiply_fusion = f32[2560,1024]{1,0:T(8,128)} fusion(f32[2560,256]{1,0:T(8,128)} %bitcast_multiply_fusion, f32[1024]{0:T(1024)S(1)} %get-tuple-element.24, f32[2560]{0:T(1024)S(1)} %add.168, f32[512,256]{1,0:T(8,128)} %copy-done.15, f32[512,256]{1,0:T(8,128)S(1)} %copy-done.14), kind=kOutput, calls=%fused_computation.5 | convolution fusion | flops 8074297344 | bytes 14170112 | tf_op jit(solution)/shard_map/dot_general | solution.py:10
  297.4 14.3 %reshape.264 = f32[5,512,2,512]{3,2,1,0:T(2,128)} reshape(f32[2560,1024]{1,0:T(8,128)} %exponential_multiply_fusion) | data formatting | bytes 20971520 | tf_op jit(solution)/shard_map/reshape | solution.py:65
  311.7 13.8 %fusion.133 = (f32[5,512,1,512]{3,2,1,0:T(1,128)}, f32[5,512,1,512]{3,2,1,0:T(1,128)S(1)}) fusion(f32[5,512,2,512]{3,2,1,0:T(2,128)} %reshape.264), kind=kLoop, calls=%fused_computation.240 | loop fusion | bytes 20971520 | tf_op jit(solution)/shard_map/slice | solution.py:71
  331.2 3.6 fusion.13
  334.9 11.5 %fusion.4 = f32[3072,512]{1,0:T(8,128)S(1)} fusion(f32[2560,512]{1,0:T(8,128)S(1)} %fusion.13, f32[512,512]{1,0:T(8,128)S(1)} %copy-done.9, f32[128,512]{1,0:T(8,128)S(1)} %copy-done.16, f32[128,512]{1,0:T(8,128)S(1)} %fusion.108, f32[128,512]{1,0:T(8,128)S(1)} %fusion.110, f32[128,512]{1,0:T(8,128)S(1)} %fusion.85), kind=kOutput, calls=%fused_computation.10 | convolution fusion | flops 9666035712 | bytes 13631488 | tf_op jit(solution)/shard_map/dot_general | solution.py:10
  356.0 11.7 %cholesky.358 = f32[128,128]{1,0:T(8,128)S(1)} custom-call(f32[128,128]{1,0:T(8,128)S(1)} %cholesky.439), custom_call_target="Cholesky" | custom-call | tf_op jit(solution)/shard_map/jit(cholesky)/cholesky | solution.py:26
  367.9 9.8 %custom-call.31 = f32[1,128,128]{1,2,0:T(8,128)S(1)} custom-call(f32[1,128,128]{2,1,0:T(8,128)S(1)} %get-tuple-element.72), custom_call_target="InvertDiagBlocksLowerTriangular" | custom-call | tf_op jit(solution)/shard_map/jit(cholesky)/cholesky | solution.py:26
  380.2 12.1 %cholesky.377 = f32[128,128]{1,0:T(8,128)S(1)} custom-call(f32[128,128]{1,0:T(8,128)S(1)} %cholesky.443), custom_call_target="Cholesky" | custom-call | tf_op jit(solution)/shard_map/jit(cholesky)/cholesky | solution.py:26
  393.7 9.8 %custom-call.32 = f32[1,128,128]{1,2,0:T(8,128)S(1)} custom-call(f32[1,128,128]{2,1,0:T(8,128)S(1)} %get-tuple-element.69), custom_call_target="InvertDiagBlocksLowerTriangular" | custom-call | tf_op jit(solution)/shard_map/jit(cholesky)/cholesky | solution.py:26
  405.1 11.7 %cholesky.398 = f32[128,128]{1,0:T(8,128)S(1)} custom-call(f32[128,128]{1,0:T(8,128)S(1)} %cholesky.448), custom_call_target="Cholesky" | custom-call | tf_op jit(solution)/shard_map/jit(cholesky)/cholesky | solution.py:26
  417.4 9.8 %custom-call.33 = f32[1,128,128]{1,2,0:T(8,128)S(1)} custom-call(f32[1,128,128]{2,1,0:T(8,128)S(1)} %get-tuple-element.66), custom_call_target="InvertDiagBlocksLowerTriangular" | custom-call | tf_op jit(solution)/shard_map/jit(cholesky)/cholesky | solution.py:26
  428.7 11.9 %cholesky.415 = f32[128,128]{1,0:T(8,128)S(1)} custom-call(f32[128,128]{1,0:T(8,128)S(1)} %convolution_subtract_fusion.11), custom_call_target="Cholesky" | custom-call | tf_op jit(solution)/shard_map/jit(cholesky)/cholesky | solution.py:26
  445.3 11.6 %while.5 = (s32[]{:T(128)}, f32[512,512]{1,0:T(8,128)}, s32[4,2]{0,1:T(2,128)S(1)}, f32[4,128,128]{2,1,0:T(8,128)S(1)}, s32[]{:T(128)}) while((s32[]{:T(128)}, f32[512,512]{1,0:T(8,128)}, s32[4,2]{0,1:T(2,128)S(1)}, f32[4,128,128]{2,1,0:T(8,128)S(1)}, s32[]{:T(128)}) %tuple.77), condition=%wide.while_cond.clone, body=%wide.while_body.clone.sunk | while | flops 2 | bytes 131181 | solution.py:28
  456.8 39.3 %custom-call.34 = f32[4,128,128]{1,2,0:T(8,128)S(1)} custom-call(f32[4,128,128]{2,1,0:T(8,128)S(1)} %get-tuple-element.22), custom_call_target="InvertDiagBlocksLowerTriangular" | custom-call | tf_op jit(solution)/shard_map/jit(_solve_triangular)/triangular_solve | solution.py:28
  507.5 11.0 %fusion.48 = f32[5,512,512]{2,1,0:T(8,128)S(1)} fusion(f32[5,512,512]{2,1,0:T(8,128)S(1)} %bitcast.195, f32[3072,512]{1,0:T(8,128)} %copy-done.1), kind=kOutput, calls=%fused_computation.90 | convolution fusion | flops 8053063680 | bytes 11534336 | tf_op jit(solution)/shard_map/dot_general | solution.py:10
  518.6 9.8 %select_select_fusion = f32[5,512,512]{2,1,0:T(8,128)S(1)} fusion(f32[5,512,1,512]{3,2,1,0:T(1,128)S(1)} %bitcast.198, f32[5,512,512]{2,1,0:T(8,128)S(1)} %fusion.48, f32[512,512]{1,0:T(8,128)S(1)} %copy-done.19, f32[512,512]{1,0:T(8,128)S(1)} %copy-done.18, pred[5]{0:T(512)(128)(4,1)S(1)} %get-tuple-element.89, pred[5]{0:T(512)(128)(4,1)S(1)} %get-tuple-element.88, ...), kind=kOutput, calls=%fused_computation.23 | convolution fusion | flops 8063025152 | bytes 18874388 | tf_op jit(solution)/shard_map/dot_general | solution.py:10
  535.6 5.8 %exponential_multiply_fusion.1 = f32[512,2048]{1,0:T(8,128)S(1)} fusion(f32[2048,256]{1,0:T(8,128)S(1)} %bitcast.196, f32[2048]{0:T(1024)S(1)} %bitcast.207, f32[512]{0:T(512)S(1)} %fusion.72, f32[512,256]{1,0:T(8,128)S(1)} %copy-done.8, f32[256]{0:T(256)S(1)} %copy-done.21), kind=kOutput, calls=%fused_computation.33 | convolution fusion | flops 3229745152 | bytes 6827008 | tf_op jit(solution)/shard_map/dot_general | solution.py:10
  541.5 15.7 %fusion.21 = f32[1,4,1,512,512]{4,3,2,1,0:T(8,128)} fusion(f32[64,4,8,512]{3,2,1,0:T(8,128)S(1)} %bitcast.208, f32[512,512]{1,0:T(8,128)S(1)} %copy-done.17, f32[512,512]{1,0:T(8,128)S(1)} %slice_bitcast_fusion, f32[512,512]{1,0:T(8,128)S(1)} %slice_bitcast_fusion.1, pred[4]{0:T(512)(128)(4,1)S(1)} %get-tuple-element.95, ...), kind=kOutput, calls=%fused_computation.32 | convolution fusion | flops 12894863360 | bytes 19922964 | tf_op jit(solution)/shard_map/dot_general | solution.py:10
  (181 shorter events, 104.4 us)
Async XLA Ops:
  6.5 80.5 %copy-start = (s32[32]{0:T(128)S(1)}, s32[32]{0:T(128)}, u32[]{:S(2)}) copy-start(s32[32]{0:T(128)} %param.10) | copy-start | bytes 388
  6.5 81.1 %copy-start.22 = (f32[512]{0:T(512)S(1)}, f32[512]{0:T(512)}, u32[]{:S(2)}) copy-start(f32[512]{0:T(512)} %param.8) | copy-start | bytes 6148
  6.5 83.3 %copy-start.6 = (f32[512,256]{1,0:T(8,128)S(1)}, f32[512,256]{1,0:T(8,128)}, u32[]{:S(2)}) copy-start(f32[512,256]{1,0:T(8,128)} %param.7) | copy-start | bytes 1572868
  6.5 83.4 %copy-start.21 = (f32[256]{0:T(256)S(1)}, f32[256]{0:T(256)}, u32[]{:S(2)}) copy-start(f32[256]{0:T(256)} %param.9) | copy-start | bytes 3076
  6.5 28.2 %all-to-all-start = ((f32[32,16,256]{2,1,0:T(8,128)}), f32[32,16,256]{2,1,0:T(8,128)S(1)}, u32[]{:S(2)}, u32[]{:S(2)}) async-start(f32[32,16,256]{2,1,0:T(8,128)} %bitcast.199), calls=%async_computation | async-start | bytes 1048576 | tf_op jit(solution)/shard_map/all_to_all | solution.py:42
  18.0 94.4 %all-gather.3.cloned.1.call-start = ((), (), s32[]{:S(2)}) async-start(), calls=%async_computation.1 | async-start | bytes 3244032 | tf_op jit(solution)/shard_map/all_gather | solution.py:47
  113.6 6.1 %copy-start.13 = (f32[512,256]{1,0:T(8,128)}, f32[512,256]{1,0:T(8,128)S(1)}, u32[]{:S(2)}) copy-start(f32[512,256]{1,0:T(8,128)S(1)} %get-tuple-element.57) | copy-start | bytes 1572868
  113.6 6.1 %copy-start.15 = (f32[512,256]{1,0:T(8,128)}, f32[512,256]{1,0:T(8,128)S(1)}, u32[]{:S(2)}) copy-start(f32[512,256]{1,0:T(8,128)S(1)} %get-tuple-element.58) | copy-start | bytes 1572868
  119.7 2.6 copy-start.12
  123.0 1.0 copy-start.11
  263.8 4.2 copy-start.20
  268.4 9.0 %copy-start.7 = (f32[512,256]{1,0:T(8,128)S(1)}, f32[512,256]{1,0:T(8,128)}, u32[]{:S(2)}) copy-start(f32[512,256]{1,0:T(8,128)} %param.7) | copy-start | bytes 1572868
  277.4 2.2 copy-start.3
  277.9 1.7 copy-start.14
  331.2 3.7 copy-start.9
  331.2 3.7 copy-start.16
  346.5 2.6 copy-start.1
  355.0 1.0 copy-start.10
  500.8 17.7 %slice-start.1 = ((s8[5242880]{0:T(1024)(128)(4,1)}), s8[4194304]{0:T(1024)(128)(4,1)S(1)}, s32[]{:S(2)}) async-start(s8[5242880]{0:T(1024)(128)(4,1)} %bitcast.197), calls=%async_computation.3 | async-start | bytes 8388608
  503.8 14.7 %slice-start.2 = ((s8[5242880]{0:T(1024)(128)(4,1)}), s8[1048576]{0:T(1024)(128)(4,1)S(1)}, s32[]{:S(2)}) async-start(s8[5242880]{0:T(1024)(128)(4,1)} %bitcast.197), calls=%async_computation.4 | async-start | bytes 2097152
  507.5 11.1 %copy-start.18 = (f32[512,512]{1,0:T(8,128)S(1)}, f32[512,512]{1,0:T(8,128)}, u32[]{:S(2)}) copy-start(f32[512,512]{1,0:T(8,128)} %copy.44) | copy-start | bytes 3145732
  507.5 11.1 %copy-start.19 = (f32[512,512]{1,0:T(8,128)S(1)}, f32[512,512]{1,0:T(8,128)}, u32[]{:S(2)}) copy-start(f32[512,512]{1,0:T(8,128)} %get-tuple-element.42) | copy-start | bytes 3145732
  528.3 2.3 copy-start.5
  532.1 2.7 copy-start.2
  532.1 3.2 copy-start.4
  532.1 3.6 copy-start.8
  535.6 5.8 %slice-start = ((f32[5,512,512]{2,1,0:T(8,128)}), f32[4,512,512]{2,1,0:T(8,128)S(1)}, s32[]{:S(2)}) async-start(f32[5,512,512]{2,1,0:T(8,128)} %copy-done.2), calls=%async_computation.2 | async-start | bytes 8388608 | tf_op jit(solution)/shard_map/slice | solution.py:95
  535.6 5.8 %slice-start.3 = ((f32[5,512,512]{2,1,0:T(8,128)}), f32[4,512,512]{2,1,0:T(8,128)S(1)}, s32[]{:S(2)}) async-start(f32[5,512,512]{2,1,0:T(8,128)} %copy-done.5), calls=%async_computation.5 | async-start | bytes 8388608 | tf_op jit(solution)/shard_map/slice | solution.py:95
  535.6 5.8 %copy-start.17 = (f32[512,512]{1,0:T(8,128)S(1)}, f32[512,512]{1,0:T(8,128)}, u32[]{:S(2)}) copy-start(f32[512,512]{1,0:T(8,128)} %copy.59) | copy-start | bytes 3145732
Sparse Core Ops, SparseCore 0:
  35.5 76.7 all-gather.2

commit v2 on v1

--- a/solution.py
+++ b/solution.py
@@ -2,6 +2,8 @@
 import jax.numpy as jnp
 from jax import lax
 from jax.sharding import PartitionSpec as P
+from jax.experimental import pallas as pl
+from jax.experimental.pallas import tpu as pltpu
 
 HI = lax.Precision.HIGHEST
 
@@ -22,10 +24,73 @@
     return (1.0 + dist) * jnp.exp(-dist)
 
 
+BASE = 128
+PHASE = 32
+
+
+def _chol_base_kernel(a_ref, l_ref, m_ref, w_ref):
+    n = a_ref.shape[0]
+    w_ref[...] = a_ref[...]
+    rows = lax.broadcasted_iota(jnp.int32, (n, n), 0)
+    lanes = lax.broadcasted_iota(jnp.int32, (n, n), 1)
+    m_ref[...] = jnp.where(rows == lanes, 1.0, 0.0).astype(jnp.float32)
+    lane1 = lax.broadcasted_iota(jnp.int32, (1, n), 1)
+    for q in range(n // PHASE):
+        lo = q * PHASE
+        size = n - lo
+        sub_rows = lax.broadcasted_iota(jnp.int32, (size, 1), 0) + lo
+        sub_lanes = lax.broadcasted_iota(jnp.int32, (size, n), 1)
+
+        def step(j, carry, lo=lo, size=size, sub_rows=sub_rows, sub_lanes=sub_lanes):
+            wrow = w_ref[pl.ds(j, 1), :]
+            piv = jnp.sum(jnp.where(lane1 == j, wrow, 0.0), axis=1, keepdims=True)
+            rs = lax.rsqrt(piv)
+            lrow = jnp.where(lane1 >= j, wrow * rs, 0.0)
+            w = w_ref[pl.ds(lo, size), :]
+            wcol = jnp.sum(jnp.where(sub_lanes == j, w, 0.0), axis=1, keepdims=True)
+            lcol = jnp.where(sub_rows > j, wcol * rs, 0.0)
+            w_ref[pl.ds(lo, size), :] = w - lcol * lrow
+            w_ref[pl.ds(j, 1), :] = lrow
+            grow = m_ref[pl.ds(j, 1), :] * rs
+            g = m_ref[pl.ds(lo, size), :]
+            m_ref[pl.ds(lo, size), :] = g - lcol * grow
+            m_ref[pl.ds(j, 1), :] = grow
+            return carry
+
+        lax.fori_loop(lo, lo + PHASE, step, 0)
+    lt = jnp.where(lanes >= rows, w_ref[...], 0.0)
+    l_ref[...] = lt.T
+    m_ref[...] = jnp.where(rows >= lanes, m_ref[...], 0.0)
+
+
+def chol_base(a):
+    n = a.shape[0]
+    return pl.pallas_call(
+        _chol_base_kernel,
+        out_shape=(
+            jax.ShapeDtypeStruct((n, n), jnp.float32),
+            jax.ShapeDtypeStruct((n, n), jnp.float32),
+        ),
+        scratch_shapes=[pltpu.VMEM((n, n), jnp.float32)],
+    )(a)
+
+
+def dot(a, b):
+    return jnp.dot(a, b, precision=HI, preferred_element_type=jnp.float32)
+
+
 def chol_inv(a):
-    low = jnp.linalg.cholesky(a)
-    eye = jnp.eye(a.shape[0], dtype=a.dtype)
-    inv = jax.scipy.linalg.solve_triangular(low, eye, lower=True)
+    n = a.shape[0]
+    if n <= BASE:
+        return chol_base(a)
+    h = n // 2
+    l11, m11 = chol_inv(a[:h, :h])
+    l21 = mm(a[h:, :h], m11)
+    l22, m22 = chol_inv(a[h:, h:] - mm(l21, l21))
+    m21 = -dot(dot(m22, l21), m11)
+    zero = jnp.zeros((h, n - h), jnp.float32)
+    low = jnp.concatenate([jnp.concatenate([l11, zero], 1), jnp.concatenate([l21, l22], 1)], 0)
+    inv = jnp.concatenate([jnp.concatenate([m11, zero], 1), jnp.concatenate([m21, m22], 1)], 0)
     return low, inv
 
 

time: 575 us -> 420 us (0.73)
  other arithmetic: 259 us -> 25.8 us
  Pallas kernels: 0 us -> 116 us
  local copies, waits for them, and re-layouts: 79.1 us -> 55.2 us
  waiting for transfers between devices: 38.8 us -> 32.9 us
    another operation x34 -> x0, other arithmetic: 240 us -> none  [the longest x29 159 us: chol_inv(): low = jnp.linalg.cholesky(a)]
    pallas_call x0 -> x8, Pallas kernels: none -> 116 us  [chol_base(): pl.pallas_call(_chol_base_kernel, out_shape=(jax.ShapeDtypeStruct((n, n),...]
    another operation x26 -> x0, matrix products: 27.5 us -> none  [the longest x14 16.6 us: chol_inv(): inv = jax.scipy.linalg.solve_triangular(low, eye, lower=True)]
    another operation x35 -> x0, local copies, waits for them, and re-layouts: 23.6 us -> none  [the longest x27 23.4 us: chol_inv(): inv = jax.scipy.linalg.solve_triangular(low, eye, lower=True)]
    dot_general x8 -> x20, matrix products: 80.4 us -> 95.2 us  [mm(): lax.dot_general(a, b, (((1,), (1,)), ((), ())), precision=HI, preferred_e...]
    dot_general x0 -> x12, matrix products: none -> 12.8 us  [dot(): return jnp.dot(a, b, precision=HI, preferred_element_type=jnp.float32)]
    all_gather x1, waiting for transfers between devices: 22.2 us -> 16.2 us  [body(): tiles_x = lax.all_gather(sel, 'row', axis=1, tiled=True)]
    unnamed x52 -> x116, local copies, waits for them, and re-layouts: 14.4 us -> 12.6 us
  transfers between devices with their start and end apart: 2 -> 2, of which waited for: 2 -> 2; matrix products, arithmetic and copies ran while one was open for 1% -> 3% of each run, Pallas kernels for 0% -> 0%
where the time goes in v2:
time: 420 us; the launch traced here: 412 us
  Pallas kernels  116 us (28%)
  matrix products  108 us (26%)
  local copies, waits for them, and re-layouts  55.2 us (13%)
  blocking collectives  48.5 us (12%)
  waiting for transfers between devices  32.9 us (8%)
  other arithmetic  25.8 us (6%)
  between operations  14.6 us (3%)
  starting transfers between devices  11.5 us (3%)
    pallas_call x8, Pallas kernels, chol_base(): pl.pallas_call(_chol_base_kernel, out_shape=(jax.ShapeDtypeStruct((n, n),...  116 us
    dot_general x20, matrix products, mm(): lax.dot_general(a, b, (((1,), (1,)), ((), ())), precision=HI, preferred_e...  95.2 us
    all_gather x1, blocking collectives, body(): nug = lax.all_gather(nugget, 'row', tiled=True)  48.5 us
    all_to_all x1, waiting for transfers between devices, body(): recv = lax.all_to_all(chunks, 'row', 0, 0, tiled=True)  16.6 us
    all_gather x1, waiting for transfers between devices, body(): tiles_x = lax.all_gather(sel, 'row', axis=1, tiled=True)  16.2 us
    reshape x1, local copies, waits for them, and re-layouts, body(): kr = kernel_tile(xr_all, x01, weights).reshape(nr, tile, 2, tile)  14.3 us
    slice x1, local copies, waits for them, and re-layouts, body(): ar1 = jnp.where(keep1, kr[:, :, 1], 0.0)  13.4 us
    dot_general x12, matrix products, dot(): return jnp.dot(a, b, precision=HI, preferred_element_type=jnp.float32)  12.8 us
  transfers between devices with their start and end apart: 2, of which 2 were waited for; matrix products, arithmetic and copies ran while one was open for 3% of the time, Pallas kernels for 0%

profile of v2, /device:TPU:8, one launch (start us, length us, event | category | flops | bytes accessed | tf_op | source)
XLA Modules:
  0.0 412.0 jit_solution(2770537917423214254)
XLA Ops:
  6.5 11.4 %all-to-all-start = ((f32[32,16,256]{2,1,0:T(8,128)}), f32[32,16,256]{2,1,0:T(8,128)S(1)}, u32[]{:S(2)}, u32[]{:S(2)}) async-start(f32[32,16,256]{2,1,0:T(8,128)} %bitcast.139), calls=%async_computation | async-start | bytes 1048576 | tf_op jit(solution)/shard_map/all_to_all | solution.py:107
  18.0 16.6 %all-to-all-done = f32[32,16,256]{2,1,0:T(8,128)S(1)} async-done(((f32[32,16,256]{2,1,0:T(8,128)}), f32[32,16,256]{2,1,0:T(8,128)S(1)}, u32[]{:S(2)}, u32[]{:S(2)}) %all-to-all-start) | async-done | bytes 524320 | tf_op jit(solution)/shard_map/all_to_all | solution.py:107
  40.6 48.5 %all-gather = f32[32,1,512]{2,1,0:T(1,128)S(1)} all-gather(f32[1,1,512]{2,1,0:T(1,128)} %bitcast.145), channel_id=1, replica_groups=mesh['row'=32,'col'=8] {'row'}, dimensions={0}, use_global_device_ids=true | all-gather | bytes 67584 | tf_op jit(solution)/shard_map/all_gather | solution.py:113
  91.5 1.8 fusion.69
  93.3 1.8 fusion.59
  96.2 16.2 %all-gather.3.cloned.1.call-done = f32[6,512,256]{2,1,0:T(8,128)} async-done(((f32[6,16,256]{2,1,0:T(8,128)}), f32[6,512,256]{2,1,0:T(8,128)}) %all-gather.3.cloned.1.call-update) | async-done | bytes 3145744 | tf_op jit(solution)/shard_map/all_gather | solution.py:112
  114.0 5.7 %exponential_multiply_fusion.2 = f32[1024,1024]{1,0:T(8,128)S(1)} fusion(f32[1024]{0:T(1024)S(1)} %get-tuple-element.38, f32[1024]{0:T(1024)S(1)} %get-tuple-element.37, f32[256]{0:T(256)S(1)} %copy-done.36, f32[512,256]{1,0:T(8,128)S(1)} %get-tuple-element.48, f32[512,256]{1,0:T(8,128)S(1)} %get-tuple-element.47), kind=kOutput, calls=%fused_computation.30 | convolution fusion | flops 3230400512 | bytes 5252096 | tf_op jit(solution)/shard_map/dot_general | solution.py:12
  119.8 2.0 copy-done.7
  124.2 14.6 %shard_map.46 = (f32[128,128]{1,0:T(8,128)}, f32[128,128]{1,0:T(8,128)}) custom-call(f32[128,128]{1,0:T(8,128)} %slice.154.a_ref), custom_call_target="tpu_custom_call" | custom-call | tf_op jit(solution)/shard_map/pallas_call | solution.py:68
  141.6 14.4 %shard_map.47 = (f32[128,128]{1,0:T(8,128)}, f32[128,128]{1,0:T(8,128)}) custom-call(f32[128,128]{1,0:T(8,128)} %convolution_subtract_fusion.6.a_ref), custom_call_target="tpu_custom_call" | custom-call | tf_op jit(solution)/shard_map/pallas_call | solution.py:68
  160.8 14.4 %shard_map.48 = (f32[128,128]{1,0:T(8,128)}, f32[128,128]{1,0:T(8,128)}) custom-call(f32[128,128]{1,0:T(8,128)} %slice.159.a_ref), custom_call_target="tpu_custom_call" | custom-call | tf_op jit(solution)/shard_map/pallas_call | solution.py:68
  177.2 14.4 %shard_map.49 = (f32[128,128]{1,0:T(8,128)}, f32[128,128]{1,0:T(8,128)}) custom-call(f32[128,128]{1,0:T(8,128)} %convolution_subtract_fusion.5.a_ref), custom_call_target="tpu_custom_call" | custom-call | tf_op jit(solution)/shard_map/pallas_call | solution.py:68
  196.4 2.6 multiply_reduce_fusion
  202.5 17.7 %exponential_multiply_fusion = f32[2560,1024]{1,0:T(8,128)} fusion(f32[2560,256]{1,0:T(8,128)} %bitcast_multiply_fusion, f32[1024]{0:T(1024)} %copy-done.44, f32[2560]{0:T(1024)} %add.160, f32[512,256]{1,0:T(8,128)} %copy-done.9, f32[512,256]{1,0:T(8,128)} %copy-done.8), kind=kOutput, calls=%fused_computation.1 | convolution fusion | flops 8074297344 | bytes 14170112 | tf_op jit(solution)/shard_map/dot_general | solution.py:12
  220.2 14.3 %reshape.233 = f32[5,512,2,512]{3,2,1,0:T(2,128)} reshape(f32[2560,1024]{1,0:T(8,128)} %exponential_multiply_fusion) | data formatting | bytes 20971520 | tf_op jit(solution)/shard_map/reshape | solution.py:130
  234.5 13.4 %fusion.113 = (f32[5,512,1,512]{3,2,1,0:T(1,128)}, f32[5,512,1,512]{3,2,1,0:T(1,128)S(1)}) fusion(f32[5,512,2,512]{3,2,1,0:T(2,128)} %reshape.233), kind=kLoop, calls=%fused_computation.177 | loop fusion | bytes 20971520 | tf_op jit(solution)/shard_map/slice | solution.py:136
  251.0 11.5 %fusion.4 = f32[3072,512]{1,0:T(8,128)S(1)} fusion(f32[2560,512]{1,0:T(8,128)S(1)} %fusion.13, f32[512,512]{1,0:T(8,128)S(1)} %copy-done.4, f32[256,256]{1,0:T(8,128)S(1)} %get-tuple-element.65, f32[128,128]{1,0:T(8,128)S(1)} %copy-done.18, f32[128,128]{1,0:T(8,128)S(1)} %copy-done.20, f32[128,256]{1,0:T(8,128)S(1)} %concatenate.197, ...), kind=kOutput, calls=%fused_computation.6 | convolution fusion | flops 9666822144 | bytes 13369344 | tf_op jit(solution)/shard_map/dot_general | solution.py:12
  262.5 2.6 copy-done
  265.1 3.1 convolution_subtract_fusion
  269.8 14.4 %shard_map.50 = (f32[128,128]{1,0:T(8,128)}, f32[128,128]{1,0:T(8,128)}) custom-call(f32[128,128]{1,0:T(8,128)} %slice.167.a_ref), custom_call_target="tpu_custom_call" | custom-call | tf_op jit(solution)/shard_map/pallas_call | solution.py:68
  285.4 1.7 convolution_subtract_fusion.4.a_ref
  287.1 14.4 %shard_map.51 = (f32[128,128]{1,0:T(8,128)}, f32[128,128]{1,0:T(8,128)}) custom-call(f32[128,128]{1,0:T(8,128)} %convolution_subtract_fusion.4.a_ref), custom_call_target="tpu_custom_call" | custom-call | tf_op jit(solution)/shard_map/pallas_call | solution.py:68
  308.1 14.4 %shard_map.52 = (f32[128,128]{1,0:T(8,128)}, f32[128,128]{1,0:T(8,128)}) custom-call(f32[128,128]{1,0:T(8,128)} %slice.172.a_ref), custom_call_target="tpu_custom_call" | custom-call | tf_op jit(solution)/shard_map/pallas_call | solution.py:68
  326.7 1.8 convolution_subtract_fusion.3.a_ref
  331.8 14.4 %shard_map.53 = (f32[128,128]{1,0:T(8,128)}, f32[128,128]{1,0:T(8,128)}) custom-call(f32[128,128]{1,0:T(8,128)} %convolution_subtract_fusion.3.a_ref), custom_call_target="tpu_custom_call" | custom-call | tf_op jit(solution)/shard_map/pallas_call | solution.py:68
  352.2 3.6 bitcast_select_fusion.2
  356.0 10.6 %fusion.57 = f32[5,512,512]{2,1,0:T(8,128)S(1)} fusion(f32[5,512,512]{2,1,0:T(8,128)S(1)} %bitcast.135, f32[3072,512]{1,0:T(8,128)} %copy-done), kind=kOutput, calls=%fused_computation.96 | convolution fusion | flops 8053063680 | bytes 11534336 | tf_op jit(solution)/shard_map/dot_general | solution.py:12
  366.9 10.1 %select_select_fusion = f32[5,512,512]{2,1,0:T(8,128)S(1)} fusion(f32[5,512,1,512]{3,2,1,0:T(1,128)S(1)} %bitcast.138, f32[5,512,512]{2,1,0:T(8,128)S(1)} %fusion.57, f32[512,512]{1,0:T(8,128)S(1)} %fusion.35, f32[512,512]{1,0:T(8,128)S(1)} %copy-done.14, pred[5]{0:T(512)(128)(4,1)S(1)} %copy-done.50, pred[5]{0:T(512)(128)(4,1)S(1)} %copy-done.49, ...), kind=kOutput, calls=%fused_computation.19 | convolution fusion | flops 8063811584 | bytes 18612244 | tf_op jit(solution)/shard_map/dot_general | solution.py:12
  377.0 2.3 copy-done.2
  380.7 2.3 copy-done.1
  383.2 6.0 %exponential_multiply_fusion.1 = f32[512,2048]{1,0:T(8,128)S(1)} fusion(f32[2048,256]{1,0:T(8,128)S(1)} %bitcast.136, f32[2048]{0:T(1024)S(1)} %bitcast.147, f32[512]{0:T(512)S(1)} %copy-done.45, f32[512,256]{1,0:T(8,128)S(1)} %copy-done.3, f32[256]{0:T(256)S(1)} %copy-done.38), kind=kOutput, calls=%fused_computation.29 | convolution fusion | flops 3229745152 | bytes 6827008 | tf_op jit(solution)/shard_map/dot_general | solution.py:12
  389.3 15.7 %fusion.21 = f32[1,4,1,512,512]{4,3,2,1,0:T(8,128)} fusion(f32[64,4,8,512]{3,2,1,0:T(8,128)S(1)} %bitcast.148, f32[512,512]{1,0:T(8,128)S(1)} %copy-done.13, f32[512,512]{1,0:T(8,128)S(1)} %slice_bitcast_fusion, f32[512,512]{1,0:T(8,128)S(1)} %slice_bitcast_fusion.1, pred[4]{0:T(512)(128)(4,1)S(1)} %copy-done.46, pred[4]{0:T(512)(128)(4,1)S(1)} %copy-done.51, ...), kind=kOutput, calls=%fused_computation.28 | convolution fusion | flops 12894863360 | bytes 19922964 | tf_op jit(solution)/shard_map/dot_general | solution.py:12
  (188 shorter events, 58.4 us)
Async XLA Ops:
  6.5 107.1 %copy-start.36 = (f32[256]{0:T(256)S(1)}, f32[256]{0:T(256)}, u32[]{:S(2)}) copy-start(f32[256]{0:T(256)} %param.6) | copy-start | bytes 3076
  6.5 28.2 %all-to-all-start = ((f32[32,16,256]{2,1,0:T(8,128)}), f32[32,16,256]{2,1,0:T(8,128)S(1)}, u32[]{:S(2)}, u32[]{:S(2)}) async-start(f32[32,16,256]{2,1,0:T(8,128)} %bitcast.139), calls=%async_computation | async-start | bytes 1048576 | tf_op jit(solution)/shard_map/all_to_all | solution.py:107
  18.0 94.4 %all-gather.3.cloned.1.call-start = ((), (), s32[]{:S(2)}) async-start(), calls=%async_computation.1 | async-start | bytes 3244032 | tf_op jit(solution)/shard_map/all_gather | solution.py:112
  38.0 81.8 %copy-start.42 = (pred[5]{0:T(512)(128)(4,1)}, pred[5]{0:T(512)(128)(4,1)S(1)}, u32[]{:S(2)}) copy-start(pred[5]{0:T(512)(128)(4,1)S(1)} %get-tuple-element.57) | copy-start | bytes 19
  113.6 6.2 %copy-start.8 = (f32[512,256]{1,0:T(8,128)}, f32[512,256]{1,0:T(8,128)S(1)}, u32[]{:S(2)}) copy-start(f32[512,256]{1,0:T(8,128)S(1)} %get-tuple-element.47) | copy-start | bytes 1572868
  113.6 6.2 %copy-start.9 = (f32[512,256]{1,0:T(8,128)}, f32[512,256]{1,0:T(8,128)S(1)}, u32[]{:S(2)}) copy-start(f32[512,256]{1,0:T(8,128)S(1)} %get-tuple-element.48) | copy-start | bytes 1572868
  138.8 57.2 %copy-start.10 = (f32[128,128]{1,0:T(8,128)S(1)}, f32[128,128]{1,0:T(8,128)}, u32[]{:S(2)}) copy-start(f32[128,128]{1,0:T(8,128)} %get-tuple-element.22) | copy-start | bytes 196612
  156.0 40.0 %copy-start.15 = (f32[128,128]{1,0:T(8,128)S(1)}, f32[128,128]{1,0:T(8,128)}, u32[]{:S(2)}) copy-start(f32[128,128]{1,0:T(8,128)} %get-tuple-element.24) | copy-start | bytes 196612
  159.5 39.4 %copy-start.3 = (f32[512,256]{1,0:T(8,128)S(1)}, f32[512,256]{1,0:T(8,128)}, u32[]{:S(2)}) copy-start(f32[512,256]{1,0:T(8,128)} %param.4) | copy-start | bytes 1572868
  251.0 14.1 %copy-start.40 = (f32[1,1,512]{2,1,0:T(1,128)S(1)}, f32[1,1,512]{2,1,0:T(1,128)}, u32[]{:S(2)}) copy-start(f32[1,1,512]{2,1,0:T(1,128)} %copy-done.39) | copy-start | bytes 6148
  284.2 65.5 %copy-start.11 = (f32[128,128]{1,0:T(8,128)S(1)}, f32[128,128]{1,0:T(8,128)}, u32[]{:S(2)}) copy-start(f32[128,128]{1,0:T(8,128)} %get-tuple-element.29) | copy-start | bytes 196612
  301.6 48.2 %copy-start.16 = (f32[128,128]{1,0:T(8,128)S(1)}, f32[128,128]{1,0:T(8,128)}, u32[]{:S(2)}) copy-start(f32[128,128]{1,0:T(8,128)} %get-tuple-element.30) | copy-start | bytes 196612
  350.8 16.0 %slice-start.1 = ((s8[5242880]{0:T(1024)(128)(4,1)}), s8[4194304]{0:T(1024)(128)(4,1)S(1)}, s32[]{:S(2)}) async-start(s8[5242880]{0:T(1024)(128)(4,1)} %bitcast.137), calls=%async_computation.3 | async-start | bytes 8388608
  352.2 14.6 %slice-start.2 = ((s8[5242880]{0:T(1024)(128)(4,1)}), s8[1048576]{0:T(1024)(128)(4,1)S(1)}, s32[]{:S(2)}) async-start(s8[5242880]{0:T(1024)(128)(4,1)} %bitcast.137), calls=%async_computation.4 | async-start | bytes 2097152
  355.8 10.8 %copy-start.26 = (f32[128,128]{1,0:T(8,128)S(1)}, f32[128,128]{1,0:T(8,128)}, u32[]{:S(2)}) copy-start(f32[128,128]{1,0:T(8,128)} %copy.61) | copy-start | bytes 196612
  355.8 10.8 %copy-start.32 = (f32[128,128]{1,0:T(8,128)S(1)}, f32[128,128]{1,0:T(8,128)}, u32[]{:S(2)}) copy-start(f32[128,128]{1,0:T(8,128)} %get-tuple-element.33) | copy-start | bytes 196612
  355.8 10.8 %copy-start.33 = (f32[128,128]{1,0:T(8,128)S(1)}, f32[128,128]{1,0:T(8,128)}, u32[]{:S(2)}) copy-start(f32[128,128]{1,0:T(8,128)} %get-tuple-element.34) | copy-start | bytes 196612
  355.8 10.8 %copy-start.12 = (f32[256,256]{1,0:T(8,128)S(1)}, f32[256,256]{1,0:T(8,128)}, u32[]{:S(2)}) copy-start(f32[256,256]{1,0:T(8,128)} %copy.63) | copy-start | bytes 786436
  355.8 10.8 %copy-start.22 = (f32[128,128]{1,0:T(8,128)S(1)}, f32[128,128]{1,0:T(8,128)}, u32[]{:S(2)}) copy-start(f32[128,128]{1,0:T(8,128)} %copy.62) | copy-start | bytes 196612
  355.9 10.8 %copy-start.28 = (f32[128,128]{1,0:T(8,128)S(1)}, f32[128,128]{1,0:T(8,128)}, u32[]{:S(2)}) copy-start(f32[128,128]{1,0:T(8,128)} %get-tuple-element.35) | copy-start | bytes 196612
  355.9 10.8 %copy-start.29 = (f32[128,128]{1,0:T(8,128)S(1)}, f32[128,128]{1,0:T(8,128)}, u32[]{:S(2)}) copy-start(f32[128,128]{1,0:T(8,128)} %get-tuple-element.36) | copy-start | bytes 196612
  355.9 10.9 %copy-start.14 = (f32[512,512]{1,0:T(8,128)S(1)}, f32[512,512]{1,0:T(8,128)}, u32[]{:S(2)}) copy-start(f32[512,512]{1,0:T(8,128)} %fusion.61) | copy-start | bytes 3145732
  355.9 10.9 %copy-start.21 = (f32[128,256]{1,0:T(8,128)S(1)}, f32[128,256]{1,0:T(8,128)}, u32[]{:S(2)}) copy-start(f32[128,256]{1,0:T(8,128)} %concatenate.206) | copy-start | bytes 393220
  355.9 10.9 %copy-start.24 = (f32[128,128]{1,0:T(8,128)S(1)}, f32[128,128]{1,0:T(8,128)}, u32[]{:S(2)}) copy-start(f32[128,128]{1,0:T(8,128)} %get-tuple-element.32) | copy-start | bytes 196612
  355.9 10.9 %copy-start.25 = (f32[256,256]{1,0:T(8,128)S(1)}, f32[256,256]{1,0:T(8,128)}, u32[]{:S(2)}) copy-start(f32[256,256]{1,0:T(8,128)} %select_maximum_fusion.6) | copy-start | bytes 786436
  355.9 10.9 %copy-start.27 = (f32[256,256]{1,0:T(8,128)S(1)}, f32[256,256]{1,0:T(8,128)}, u32[]{:S(2)}) copy-start(f32[256,256]{1,0:T(8,128)} %convolution_negate_fusion) | copy-start | bytes 786436
  355.9 10.9 %copy-start.48 = (pred[5]{0:T(512)(128)(4,1)S(1)}, pred[5]{0:T(512)(128)(4,1)}, u32[]{:S(2)}) copy-start(pred[5]{0:T(512)(128)(4,1)} %get-tuple-element.56) | copy-start | bytes 19
  355.9 10.9 %copy-start.49 = (pred[5]{0:T(512)(128)(4,1)S(1)}, pred[5]{0:T(512)(128)(4,1)}, u32[]{:S(2)}) copy-start(pred[5]{0:T(512)(128)(4,1)} %get-tuple-element.58) | copy-start | bytes 19
  355.9 10.9 %copy-start.50 = (pred[5]{0:T(512)(128)(4,1)S(1)}, pred[5]{0:T(512)(128)(4,1)}, u32[]{:S(2)}) copy-start(pred[5]{0:T(512)(128)(4,1)} %get-tuple-element.59) | copy-start | bytes 19
  356.0 10.9 %copy-start.53 = (pred[5]{0:T(512)(128)(4,1)S(1)}, pred[5]{0:T(512)(128)(4,1)}, u32[]{:S(2)}) copy-start(pred[5]{0:T(512)(128)(4,1)} %get-tuple-element.39) | copy-start | bytes 19
  383.1 6.1 %slice-start = ((f32[5,512,512]{2,1,0:T(8,128)}), f32[4,512,512]{2,1,0:T(8,128)S(1)}, s32[]{:S(2)}) async-start(f32[5,512,512]{2,1,0:T(8,128)} %copy-done.1), calls=%async_computation.2 | async-start | bytes 8388608 | tf_op jit(solution)/shard_map/slice | solution.py:160
  383.1 6.1 %slice-start.3 = ((f32[5,512,512]{2,1,0:T(8,128)}), f32[4,512,512]{2,1,0:T(8,128)S(1)}, s32[]{:S(2)}) async-start(f32[5,512,512]{2,1,0:T(8,128)} %copy-done.2), calls=%async_computation.5 | async-start | bytes 8388608 | tf_op jit(solution)/shard_map/slice | solution.py:160
  (29 other events, 81.5 us)
Sparse Core Ops, SparseCore 0:
  35.5 76.7 all-gather.2

commit v3 on v2

--- a/solution.py
+++ b/solution.py
@@ -8,9 +8,9 @@
 HI = lax.Precision.HIGHEST
 
 
-def mm(a, b):
+def mm(a, b, precision=HI):
     return lax.dot_general(
-        a, b, (((1,), (1,)), ((), ())), precision=HI, preferred_element_type=jnp.float32
+        a, b, (((1,), (1,)), ((), ())), precision=precision, preferred_element_type=jnp.float32
     )
 
 
@@ -18,7 +18,7 @@
     weighted = xrow * weights
     sq_row = jnp.sum(weighted * xrow, axis=1)
     sq_col = jnp.sum(xcol * xcol * weights, axis=1)
-    cross = mm(weighted, xcol)
+    cross = mm(weighted, xcol, lax.Precision.HIGH)
     dist_sq = jnp.maximum(sq_row[:, None] + sq_col[None, :] - 2.0 * cross, 0.0)
     dist = jnp.sqrt(3.0 * dist_sq)
     return (1.0 + dist) * jnp.exp(-dist)
@@ -110,10 +110,11 @@
     )[:, 0]
     sel = jnp.concatenate([recv[:2], mine], axis=0)
     tiles_x = lax.all_gather(sel, "row", axis=1, tiled=True)
-    nug = lax.all_gather(nugget, "row", tiled=True)
+    slot = jnp.arange(2, dtype=jnp.int32)[:, None] == my_row
+    nug = lax.psum(jnp.where(slot, nugget[None, :], 0.0), "row")
     x0, x1 = tiles_x[0], tiles_x[1]
     xcols = tiles_x[2:]
-    n0, n1 = nug[:tile], nug[tile : 2 * tile]
+    n0, n1 = nug[0], nug[1]
 
     cols = my_col + n_col * jnp.arange(blocks, dtype=jnp.int32)
     rows = jnp.concatenate([my_row[None], cols])
@@ -127,13 +128,13 @@
     a10 = k01[tile:, :tile]
     a11 = k01[tile:, tile:] + eye * n1[None, :]
 
-    kr = kernel_tile(xr_all, x01, weights).reshape(nr, tile, 2, tile)
+    kr = kernel_tile(xr_all, x01, weights).reshape(nr, tile, 2 * tile)
     bs = band_start[rows]
     keep0 = (bs <= 0)[:, None, None]
     keep1 = ((bs <= 1) & (rows >= 1))[:, None, None]
-    ar0 = jnp.where(keep0, kr[:, :, 0], 0.0)
+    ar0 = jnp.where(keep0, kr[:, :, :tile], 0.0)
     ar0 = ar0 + jnp.where((rows == 0)[:, None, None], eye * n0[None, :], 0.0)
-    ar1 = jnp.where(keep1, kr[:, :, 1], 0.0)
+    ar1 = jnp.where(keep1, kr[:, :, tile:], 0.0)
     ar1 = ar1 + jnp.where((rows == 1)[:, None, None], eye * n1[None, :], 0.0)
 
     l00, m0 = chol_inv(a00)
@@ -158,7 +159,7 @@
     aout = aout + jnp.where((cols == my_row)[:, None, None], eye * nugget[None, :], 0.0)
     left = jnp.concatenate([lr0[0], lr1[0]], axis=1)
     right = jnp.concatenate([lr0[1:], lr1[1:]], axis=2).reshape(-1, 2 * tile)
-    prod = mm(left, right).reshape(tile, blocks, tile).transpose(1, 0, 2)
+    prod = mm(left, right, lax.Precision.HIGH).reshape(tile, blocks, tile).transpose(1, 0, 2)
     live = ((cols > 1) & (cols <= my_row))[:, None, None]
     res = aout - jnp.where(live, prod, 0.0)
     res = jnp.where((cols == 0)[:, None, None], lr0[0][None], res)

time: 420 us -> 441 us (1.050)
  blocking collectives: 48.5 us -> 72.9 us
  waiting for transfers between devices: 32.9 us -> 16.7 us
  local copies, waits for them, and re-layouts: 55.2 us -> 66.2 us
  other arithmetic: 25.8 us -> 34 us
  matrix products: 108 us -> 102 us
    psum x0 -> x1, blocking collectives: none -> 72.9 us  [body(): nug = lax.psum(jnp.where(slot, nugget[None, :], 0.0), 'row')]
    all_gather x1 -> x0, blocking collectives: 48.5 us -> none  [body(): nug = lax.all_gather(nugget, 'row', tiled=True)]
    all_gather x1, waiting for transfers between devices: 16.2 us -> 0.01 us  [body(): tiles_x = lax.all_gather(sel, 'row', axis=1, tiled=True)]
    unnamed x116 -> x101, local copies, waits for them, and re-layouts: 12.6 us -> 22.5 us
    reshape x1, local copies, waits for them, and re-layouts: 14.3 us -> 5.99 us  [body(): lr0 = sol0[tile:].reshape(nr, tile, tile)]
    slice x2, local copies, waits for them, and re-layouts: 13.4 us -> 5.76 us  [the longest x1 5.75 us: body(): ar1 = jnp.where(keep1, kr[:, :, tile:], 0.0)]
    dot_general x20, matrix products: 95.2 us -> 88.6 us  [mm(): lax.dot_general(a, b, (((1,), (1,)), ((), ())), precision=precision, pref...]
    add x0 -> x1, local copies, waits for them, and re-layouts: none -> 5.95 us  [body(): ar0 = ar0 + jnp.where((rows == 0)[:, None, None], eye * n0[None, :], 0.0)]
  transfers between devices with their start and end apart: 2 -> 2, of which waited for: 2 -> 1; matrix products, arithmetic and copies ran while one was open for 3% -> 2% of each run, Pallas kernels for 0% -> 0%
where the time goes in v3:
time: 441 us; the launch traced here: 434 us
  Pallas kernels  116 us (26%)
  matrix products  102 us (23%)
  blocking collectives  72.9 us (17%)
  local copies, waits for them, and re-layouts  66.2 us (15%)
  other arithmetic  34 us (8%)
  waiting for transfers between devices  16.7 us (4%)
  between operations  14.6 us (3%)
  starting transfers between devices  11.5 us (3%)
    pallas_call x8, Pallas kernels, chol_base(): pl.pallas_call(_chol_base_kernel, out_shape=(jax.ShapeDtypeStruct((n, n),...  116 us
    dot_general x20, matrix products, mm(): lax.dot_general(a, b, (((1,), (1,)), ((), ())), precision=precision, pref...  88.6 us
    psum x1, blocking collectives, body(): nug = lax.psum(jnp.where(slot, nugget[None, :], 0.0), 'row')  72.9 us
    unnamed x101, local copies, waits for them, and re-layouts  22.5 us
    all_to_all x1, waiting for transfers between devices, body(): recv = lax.all_to_all(chunks, 'row', 0, 0, tiled=True)  16.6 us
    dot_general x12, matrix products, dot(): return jnp.dot(a, b, precision=HI, preferred_element_type=jnp.float32)  13.6 us
    all_to_all x1, starting transfers between devices, body(): recv = lax.all_to_all(chunks, 'row', 0, 0, tiled=True)  11.4 us
    select_n x2, other arithmetic, body(): lr0 = jnp.where((rows == 0)[:, None, None], l00[None], lr0)  8.89 us
  transfers between devices with their start and end apart: 2, of which 1 were waited for; matrix products, arithmetic and copies ran while one was open for 2% of the time, Pallas kernels for 0%

profile of v3, /device:TPU:8, one launch (start us, length us, event | category | flops | bytes accessed | tf_op | source)
XLA Modules:
  0.0 433.9 jit_solution(373570991577032273)
XLA Ops:
  6.5 11.4 %all-to-all-start = ((f32[32,16,256]{2,1,0:T(8,128)}), f32[32,16,256]{2,1,0:T(8,128)S(1)}, u32[]{:S(2)}, u32[]{:S(2)}) async-start(f32[32,16,256]{2,1,0:T(8,128)} %bitcast.121), calls=%async_computation | async-start | bytes 1048576 | tf_op jit(solution)/shard_map/all_to_all | solution.py:107
  18.1 16.6 %all-to-all-done = f32[32,16,256]{2,1,0:T(8,128)S(1)} async-done(((f32[32,16,256]{2,1,0:T(8,128)}), f32[32,16,256]{2,1,0:T(8,128)S(1)}, u32[]{:S(2)}, u32[]{:S(2)}) %all-to-all-start) | async-done | bytes 524320 | tf_op jit(solution)/shard_map/all_to_all | solution.py:107
  39.4 72.9 %psum.7 = f32[2,512]{1,0:T(2,128)S(1)} all-reduce(f32[2,512]{1,0:T(2,128)S(1)} %broadcast_select_fusion.1), channel_id=1, replica_groups=mesh['row'=32,'col'=8] {'row'}, use_global_device_ids=true, to_apply=%region_2.3 | all-reduce | flops 1024 | bytes 8192 | tf_op jit(solution)/shard_map/psum | solution.py:114
  120.2 3.9 exponential_multiply_fusion.2
  128.1 14.9 %shard_map.46 = (f32[128,128]{1,0:T(8,128)}, f32[128,128]{1,0:T(8,128)}) custom-call(f32[128,128]{1,0:T(8,128)} %slice.152.a_ref), custom_call_target="tpu_custom_call" | custom-call | tf_op jit(solution)/shard_map/pallas_call | solution.py:68
  145.8 14.4 %shard_map.47 = (f32[128,128]{1,0:T(8,128)}, f32[128,128]{1,0:T(8,128)}) custom-call(f32[128,128]{1,0:T(8,128)} %convolution_subtract_fusion.6.a_ref), custom_call_target="tpu_custom_call" | custom-call | tf_op jit(solution)/shard_map/pallas_call | solution.py:68
  165.0 14.4 %shard_map.48 = (f32[128,128]{1,0:T(8,128)}, f32[128,128]{1,0:T(8,128)}) custom-call(f32[128,128]{1,0:T(8,128)} %slice.157.a_ref), custom_call_target="tpu_custom_call" | custom-call | tf_op jit(solution)/shard_map/pallas_call | solution.py:68
  181.4 14.4 %shard_map.49 = (f32[128,128]{1,0:T(8,128)}, f32[128,128]{1,0:T(8,128)}) custom-call(f32[128,128]{1,0:T(8,128)} %convolution_subtract_fusion.5.a_ref), custom_call_target="tpu_custom_call" | custom-call | tf_op jit(solution)/shard_map/pallas_call | solution.py:68
  206.8 11.0 %exponential_multiply_fusion = f32[2560,1024]{1,0:T(8,128)S(1)} fusion(f32[2560,256]{1,0:T(8,128)} %bitcast_multiply_fusion, f32[1024]{0:T(1024)S(1)} %copy-done.37, f32[2560]{0:T(1024)S(1)} %add.161, f32[512,256]{1,0:T(8,128)} %copy-done.13, f32[512,256]{1,0:T(8,128)S(1)} %copy-done.12), kind=kOutput, calls=%fused_computation.1 | convolution fusion | flops 4047765504 | bytes 14170112 | tf_op jit(solution)/shard_map/dot_general | solution.py:12
  217.8 5.8 %fusion.111 = (f32[5,512,512]{2,1,0:T(8,128)}, f32[5,512,512]{2,1,0:T(8,128)}) fusion(f32[5,512,1024]{2,1,0:T(8,128)S(1)} %bitcast.119), kind=kLoop, calls=%fused_computation.176 | loop fusion | bytes 20971520 | tf_op jit(solution)/shard_map/slice | solution.py:137
  223.5 6.0 %copy.65 = f32[5,512,512]{1,2,0:T(8,128)} copy(f32[5,512,512]{2,1,0:T(8,128)} %get-tuple-element.42) | data formatting | bytes 10485760
  229.6 5.9 %select_add_fusion = f32[5,512,512]{1,2,0:T(8,128)} fusion(f32[5,512,512]{1,2,0:T(8,128)} %copy.65, f32[512,512]{0,1:T(8,128)} %copy.39, pred[5]{0:T(512)(128)(4,1)S(1)} %copy-done.33, pred[5]{0:T(512)(128)(4,1)S(1)} %copy-done.39), kind=kLoop, calls=%fused_computation.15 | loop fusion | flops 3932160 | bytes 11534346 | tf_op jit(solution)/shard_map/add | solution.py:136
  235.6 6.0 %copy.40 = f32[5,512,512]{2,1,0:T(8,128)} copy(f32[5,512,512]{1,2,0:T(8,128)} %select_add_fusion) | data formatting | bytes 10485760 | tf_op jit(solution)/shard_map/add | solution.py:136
  243.1 12.8 %fusion.4 = f32[3072,512]{1,0:T(8,128)S(1)} fusion(f32[2560,512]{1,0:T(8,128)} %bitcast.117, f32[512,512]{1,0:T(8,128)} %get-tuple-element.46, f32[256,256]{1,0:T(8,128)S(1)} %get-tuple-element.65, f32[128,128]{1,0:T(8,128)S(1)} %copy-done.20, f32[128,128]{1,0:T(8,128)S(1)} %copy-done.22, f32[128,256]{1,0:T(8,128)S(1)} %concatenate.197, ...), kind=kOutput, calls=%fused_computation.6 | convolution fusion | flops 9666822144 | bytes 13369344 | tf_op jit(solution)/shard_map/dot_general | solution.py:12
  256.0 2.7 copy-done.1
  258.6 3.1 convolution_subtract_fusion
  263.3 14.4 %shard_map.50 = (f32[128,128]{1,0:T(8,128)}, f32[128,128]{1,0:T(8,128)}) custom-call(f32[128,128]{1,0:T(8,128)} %slice.165.a_ref), custom_call_target="tpu_custom_call" | custom-call | tf_op jit(solution)/shard_map/pallas_call | solution.py:68
  280.7 14.4 %shard_map.51 = (f32[128,128]{1,0:T(8,128)}, f32[128,128]{1,0:T(8,128)}) custom-call(f32[128,128]{1,0:T(8,128)} %convolution_subtract_fusion.4.a_ref), custom_call_target="tpu_custom_call" | custom-call | tf_op jit(solution)/shard_map/pallas_call | solution.py:68
  300.9 14.4 %shard_map.52 = (f32[128,128]{1,0:T(8,128)}, f32[128,128]{1,0:T(8,128)}) custom-call(f32[128,128]{1,0:T(8,128)} %slice.170.a_ref), custom_call_target="tpu_custom_call" | custom-call | tf_op jit(solution)/shard_map/pallas_call | solution.py:68
  324.3 14.6 %shard_map.53 = (f32[128,128]{1,0:T(8,128)}, f32[128,128]{1,0:T(8,128)}) custom-call(f32[128,128]{1,0:T(8,128)} %convolution_subtract_fusion.3.a_ref), custom_call_target="tpu_custom_call" | custom-call | tf_op jit(solution)/shard_map/pallas_call | solution.py:68
  348.2 5.6 %bitcast_select_fusion = (f32[2560,512]{1,0:T(8,128)S(1)}, f32[2560,512]{1,0:T(8,128)}) fusion(f32[512,512]{1,0:T(8,128)S(1)} %fusion.38, pred[2560]{0:T(1024)(128)(4,1)S(1)} %copy-done.31, f32[3072,512]{1,0:T(8,128)} %copy-done.1), kind=kLoop, calls=%fused_computation.10 | loop fusion | flops 1310720 | bytes 16779776 | tf_op jit(solution)/shard_map/jit(_where)/select_n | solution.py:145
  353.8 12.2 %fusion.55 = f32[5,512,512]{1,2,0:T(8,128)} fusion(f32[5,512,512]{2,1,0:T(8,128)S(1)} %bitcast.118, f32[3072,512]{1,0:T(8,128)} %copy-done.1), kind=kOutput, calls=%fused_computation.93 | convolution fusion | flops 8053063680 | bytes 11534336 | tf_op jit(solution)/shard_map/dot_general | solution.py:12
  366.0 6.0 %copy.64 = f32[5,512,512]{1,2,0:T(8,128)} copy(f32[5,512,512]{2,1,0:T(8,128)} %get-tuple-element.41) | data formatting | bytes 10485760
  372.0 14.0 %select_select_fusion = f32[5,512,512]{1,2,0:T(8,128)S(1)} fusion(f32[5,512,512]{1,2,0:T(8,128)} %fusion.55, f32[5,512,512]{1,2,0:T(8,128)} %copy.64, f32[512,512]{0,1:T(8,128)} %copy.48, f32[512,512]{0,1:T(8,128)} %copy.31, pred[5]{0:T(512)(128)(4,1)S(1)} %copy-done.44, pred[5]{0:T(512)(128)(4,1)S(1)} %copy-done.43, pred[5]{0:T(512)(128)(4,1)S(1)} %copy-done.42, ...), kind=kOutput, calls=%fused_computation.11 | convolution fusion | flops 8063811584 | bytes 18612244 | tf_op jit(solution)/shard_map/dot_general | solution.py:12
  386.0 2.3 copy-done.3
  390.8 6.0 %copy.50 = f32[5,512,512]{1,2,0:T(8,128)} copy(f32[5,512,512]{2,1,0:T(8,128)} %bitcast.116) | data formatting | bytes 10485760 | tf_op jit(solution)/shard_map/reshape | solution.py:144
  396.8 3.3 broadcast_select_fusion
  400.1 2.4 copy-done.2
  403.5 2.6 copy.49
  406.1 2.6 copy.51
  408.8 5.9 %exponential_multiply_fusion.1 = f32[512,2048]{1,0:T(8,128)} fusion(f32[2048,256]{1,0:T(8,128)S(1)} %bitcast.120, f32[2048]{0:T(1024)S(1)} %bitcast.128, f32[512]{0:T(512)S(1)} %copy-done.38, f32[512,256]{1,0:T(8,128)S(1)} %copy-done.5, f32[256]{0:T(256)S(1)} %copy-done.30), kind=kOutput, calls=%fused_computation.26 | convolution fusion | flops 1619132416 | bytes 6827008 | tf_op jit(solution)/shard_map/dot_general | solution.py:12
  414.7 11.8 %fusion.19 = f32[1,4,1,512,512]{4,3,2,1,0:T(8,128)} fusion(f32[64,4,8,512]{3,2,1,0:T(8,128)} %bitcast.129, f32[512,512]{1,0:T(8,128)} %fusion.57, f32[512,512]{1,0:T(8,128)} %copy.51, f32[512,512]{1,0:T(8,128)} %copy.49, pred[4]{0:T(512)(128)(4,1)S(1)} %copy-done.40, pred[4]{0:T(512)(128)(4,1)S(1)} %copy-done.46, pred[4]{0:T(512)(128)(4,1)S(1)} %copy-done.41, ...), kind=kOutput, calls=%fused_computation.25 | convolution fusion | flops 6452412416 | bytes 22020116 | tf_op jit(solution)/shard_map/dot_general | solution.py:12
  (179 shorter events, 70.6 us)
Async XLA Ops:
  6.5 110.2 %copy-start.4 = (f32[512,256]{1,0:T(8,128)S(1)}, f32[512,256]{1,0:T(8,128)}, u32[]{:S(2)}) copy-start(f32[512,256]{1,0:T(8,128)} %param.4) | copy-start | bytes 1572868
  6.5 107.2 %copy-start = (s32[32]{0:T(128)S(1)}, s32[32]{0:T(128)}, u32[]{:S(2)}) copy-start(s32[32]{0:T(128)} %param.7) | copy-start | bytes 388
  6.5 110.9 %copy-start.35 = (f32[512]{0:T(512)S(1)}, f32[512]{0:T(512)}, u32[]{:S(2)}) copy-start(f32[512]{0:T(512)} %param.5) | copy-start | bytes 6148
  6.5 110.2 %copy-start.30 = (f32[256]{0:T(256)S(1)}, f32[256]{0:T(256)}, u32[]{:S(2)}) copy-start(f32[256]{0:T(256)} %param.6) | copy-start | bytes 3076
  6.5 28.2 %all-to-all-start = ((f32[32,16,256]{2,1,0:T(8,128)}), f32[32,16,256]{2,1,0:T(8,128)S(1)}, u32[]{:S(2)}, u32[]{:S(2)}) async-start(f32[32,16,256]{2,1,0:T(8,128)} %bitcast.121), calls=%async_computation | async-start | bytes 1048576 | tf_op jit(solution)/shard_map/all_to_all | solution.py:107
  18.0 100.5 %all-gather.2.cloned.1.call-start = ((), (), s32[]{:S(2)}) async-start(), calls=%async_computation.1 | async-start | bytes 3244032 | tf_op jit(solution)/shard_map/all_gather | solution.py:112
  143.0 57.1 %copy-start.14 = (f32[128,128]{1,0:T(8,128)S(1)}, f32[128,128]{1,0:T(8,128)}, u32[]{:S(2)}) copy-start(f32[128,128]{1,0:T(8,128)} %get-tuple-element.22) | copy-start | bytes 196612
  160.3 39.9 %copy-start.18 = (f32[128,128]{1,0:T(8,128)S(1)}, f32[128,128]{1,0:T(8,128)}, u32[]{:S(2)}) copy-start(f32[128,128]{1,0:T(8,128)} %get-tuple-element.24) | copy-start | bytes 196612
  223.5 6.1 %copy-start.33 = (pred[5]{0:T(512)(128)(4,1)S(1)}, pred[5]{0:T(512)(128)(4,1)}, u32[]{:S(2)}) copy-start(pred[5]{0:T(512)(128)(4,1)} %copy-done.32) | copy-start | bytes 19
  223.5 6.1 %copy-start.39 = (pred[5]{0:T(512)(128)(4,1)S(1)}, pred[5]{0:T(512)(128)(4,1)}, u32[]{:S(2)}) copy-start(pred[5]{0:T(512)(128)(4,1)} %get-tuple-element.60) | copy-start | bytes 19
  235.5 6.0 %copy-start.25 = (f32[128,128]{1,0:T(8,128)S(1)}, f32[128,128]{1,0:T(8,128)}, u32[]{:S(2)}) copy-start(f32[128,128]{1,0:T(8,128)} %copy.32) | copy-start | bytes 196612
  235.5 6.0 %copy-start.29 = (f32[128,128]{1,0:T(8,128)S(1)}, f32[128,128]{1,0:T(8,128)}, u32[]{:S(2)}) copy-start(f32[128,128]{1,0:T(8,128)} %get-tuple-element.21) | copy-start | bytes 196612
  235.6 7.6 %copy-start.16 = (f32[256,256]{1,0:T(8,128)S(1)}, f32[256,256]{1,0:T(8,128)}, u32[]{:S(2)}) copy-start(f32[256,256]{1,0:T(8,128)} %convolution_negate_fusion.1) | copy-start | bytes 786436
  235.6 7.6 %copy-start.20 = (f32[128,128]{1,0:T(8,128)S(1)}, f32[128,128]{1,0:T(8,128)}, u32[]{:S(2)}) copy-start(f32[128,128]{1,0:T(8,128)} %get-tuple-element.28) | copy-start | bytes 196612
  235.6 7.6 %copy-start.22 = (f32[128,128]{1,0:T(8,128)S(1)}, f32[128,128]{1,0:T(8,128)}, u32[]{:S(2)}) copy-start(f32[128,128]{1,0:T(8,128)} %copy-done.21) | copy-start | bytes 196612
  277.7 64.7 %copy-start.15 = (f32[128,128]{1,0:T(8,128)S(1)}, f32[128,128]{1,0:T(8,128)}, u32[]{:S(2)}) copy-start(f32[128,128]{1,0:T(8,128)} %get-tuple-element.29) | copy-start | bytes 196612
  295.1 47.4 %copy-start.19 = (f32[128,128]{1,0:T(8,128)S(1)}, f32[128,128]{1,0:T(8,128)}, u32[]{:S(2)}) copy-start(f32[128,128]{1,0:T(8,128)} %get-tuple-element.30) | copy-start | bytes 196612
  317.9 29.1 %copy-start.17 = (f32[256,256]{1,0:T(8,128)S(1)}, f32[256,256]{1,0:T(8,128)}, u32[]{:S(2)}) copy-start(f32[256,256]{1,0:T(8,128)} %get-tuple-element.66) | copy-start | bytes 786436
  323.5 23.6 %copy-start.24 = (f32[128,128]{1,0:T(8,128)S(1)}, f32[128,128]{1,0:T(8,128)}, u32[]{:S(2)}) copy-start(f32[128,128]{1,0:T(8,128)} %copy.34) | copy-start | bytes 196612
  323.5 24.7 %copy-start.31 = (pred[2560]{0:T(1024)(128)(4,1)S(1)}, pred[2560]{0:T(1024)(128)(4,1)}, u32[]{:S(2)}) copy-start(pred[2560]{0:T(1024)(128)(4,1)} %broadcast_in_dim.224) | copy-start | bytes 7684
  365.9 6.0 %copy-start.23 = (f32[128,256]{1,0:T(8,128)S(1)}, f32[128,256]{1,0:T(8,128)}, u32[]{:S(2)}) copy-start(f32[128,256]{1,0:T(8,128)} %concatenate.206) | copy-start | bytes 393220
  365.9 6.0 %copy-start.26 = (f32[128,128]{1,0:T(8,128)S(1)}, f32[128,128]{1,0:T(8,128)}, u32[]{:S(2)}) copy-start(f32[128,128]{1,0:T(8,128)} %get-tuple-element.32) | copy-start | bytes 196612
  365.9 6.0 %copy-start.28 = (f32[128,128]{1,0:T(8,128)S(1)}, f32[128,128]{1,0:T(8,128)}, u32[]{:S(2)}) copy-start(f32[128,128]{1,0:T(8,128)} %copy-done.27) | copy-start | bytes 196612
  365.9 6.0 %copy-start.42 = (pred[5]{0:T(512)(128)(4,1)S(1)}, pred[5]{0:T(512)(128)(4,1)}, u32[]{:S(2)}) copy-start(pred[5]{0:T(512)(128)(4,1)} %get-tuple-element.56) | copy-start | bytes 19
  365.9 6.0 %copy-start.43 = (pred[5]{0:T(512)(128)(4,1)S(1)}, pred[5]{0:T(512)(128)(4,1)}, u32[]{:S(2)}) copy-start(pred[5]{0:T(512)(128)(4,1)} %get-tuple-element.58) | copy-start | bytes 19
  365.9 6.0 %copy-start.44 = (pred[5]{0:T(512)(128)(4,1)S(1)}, pred[5]{0:T(512)(128)(4,1)}, u32[]{:S(2)}) copy-start(pred[5]{0:T(512)(128)(4,1)} %get-tuple-element.59) | copy-start | bytes 19
  365.9 6.0 %copy-start.45 = (pred[5]{0:T(512)(128)(4,1)S(1)}, pred[5]{0:T(512)(128)(4,1)}, u32[]{:S(2)}) copy-start(pred[5]{0:T(512)(128)(4,1)} %get-tuple-element.39) | copy-start | bytes 19
  390.8 6.0 %copy-start.6 = (f32[512,512]{0,1:T(8,128)S(1)}, f32[512,512]{0,1:T(8,128)}, u32[]{:S(2)}) copy-start(f32[512,512]{0,1:T(8,128)} %copy.36) | copy-start | bytes 3145732
  390.8 6.0 %copy-start.34 = (pred[5]{0:T(512)(128)(4,1)S(1)}, pred[5]{0:T(512)(128)(4,1)}, u32[]{:S(2)}) copy-start(pred[5]{0:T(512)(128)(4,1)} %copy-done.32) | copy-start | bytes 19
  402.5 6.2 %copy-start.5 = (f32[512,256]{1,0:T(8,128)S(1)}, f32[512,256]{1,0:T(8,128)}, u32[]{:S(2)}) copy-start(f32[512,256]{1,0:T(8,128)} %param.4) | copy-start | bytes 1572868
  402.5 6.2 %copy-start.38 = (f32[512]{0:T(512)S(1)}, f32[512]{0:T(512)}, u32[]{:S(2)}) copy-start(f32[512]{0:T(512)} %fusion.67) | copy-start | bytes 6148
  408.7 6.0 %slice-start = ((f32[5,512,512]{1,2,0:T(8,128)}), f32[4,512,512]{1,2,0:T(8,128)S(1)}, s32[]{:S(2)}) async-start(f32[5,512,512]{1,2,0:T(8,128)} %copy-done.2), calls=%async_computation.2 | async-start | bytes 8388608 | tf_op jit(solution)/shard_map/slice | solution.py:161
  (21 other events, 81.8 us)
Sparse Core Ops, SparseCore 0:
  35.5 76.7 all-gather.1

commit v4 on v3

--- a/solution.py
+++ b/solution.py
@@ -103,18 +103,18 @@
     my_row = lax.axis_index("row")
     my_col = lax.axis_index("col")
 
+    slot = jnp.arange(2, dtype=jnp.int32)[:, None] == my_row
+    nug = lax.psum(jnp.where(slot, nugget[None, :], 0.0), "row")
+    n0, n1 = nug[0], nug[1]
+
     chunks = points.reshape(n_row, piece, points.shape[1])
     recv = lax.all_to_all(chunks, "row", 0, 0, tiled=True)
+    tiles01 = lax.all_gather(recv[:2], "row", axis=1, tiled=True)
     mine = lax.dynamic_slice_in_dim(
         recv.reshape(blocks, n_col, piece, points.shape[1]), my_col, 1, axis=1
     )[:, 0]
-    sel = jnp.concatenate([recv[:2], mine], axis=0)
-    tiles_x = lax.all_gather(sel, "row", axis=1, tiled=True)
-    slot = jnp.arange(2, dtype=jnp.int32)[:, None] == my_row
-    nug = lax.psum(jnp.where(slot, nugget[None, :], 0.0), "row")
-    x0, x1 = tiles_x[0], tiles_x[1]
-    xcols = tiles_x[2:]
-    n0, n1 = nug[0], nug[1]
+    xcols = lax.all_gather(mine, "row", axis=1, tiled=True)
+    x0, x1 = tiles01[0], tiles01[1]
 
     cols = my_col + n_col * jnp.arange(blocks, dtype=jnp.int32)
     rows = jnp.concatenate([my_row[None], cols])

time: 441 us -> 431 us (0.977)
    unnamed x101 -> x105, local copies, waits for them, and re-layouts: 22.5 us -> 21.8 us
  transfers between devices with their start and end apart: 2 -> 3, of which waited for: 1 -> 1; matrix products, arithmetic and copies ran while one was open for 2% -> 9% of each run, Pallas kernels for 0% -> 14%
where the time goes in v4:
time: 431 us; the launch traced here: 424 us
  Pallas kernels  116 us (27%)
  matrix products  98.9 us (23%)
  blocking collectives  72.7 us (17%)
  local copies, waits for them, and re-layouts  62.1 us (14%)
  other arithmetic  31.9 us (7%)
  waiting for transfers between devices  16.6 us (4%)
  between operations  14.6 us (3%)
  starting transfers between devices  11.5 us (3%)
    pallas_call x8, Pallas kernels, chol_base(): pl.pallas_call(_chol_base_kernel, out_shape=(jax.ShapeDtypeStruct((n, n),...  116 us
    dot_general x20, matrix products, mm(): lax.dot_general(a, b, (((1,), (1,)), ((), ())), precision=precision, pref...  88 us
    psum x1, blocking collectives, body(): nug = lax.psum(jnp.where(slot, nugget[None, :], 0.0), 'row')  72.7 us
    unnamed x105, local copies, waits for them, and re-layouts  21.8 us
    all_to_all x1, waiting for transfers between devices, body(): recv = lax.all_to_all(chunks, 'row', 0, 0, tiled=True)  16.6 us
    all_to_all x1, starting transfers between devices, body(): recv = lax.all_to_all(chunks, 'row', 0, 0, tiled=True)  11.4 us
    dot_general x12, matrix products, dot(): return jnp.dot(a, b, precision=HI, preferred_element_type=jnp.float32)  10.9 us
    select_n x2, other arithmetic, body(): lr0 = jnp.where((rows == 0)[:, None, None], l00[None], lr0)  8.87 us
  transfers between devices with their start and end apart: 3, of which 1 were waited for; matrix products, arithmetic and copies ran while one was open for 9% of the time, Pallas kernels for 14%

profile of v4, /device:TPU:8, one launch (start us, length us, event | category | flops | bytes accessed | tf_op | source)
XLA Modules:
  0.0 424.5 jit_solution(12080625777201070202)
XLA Ops:
  6.5 11.4 %all-to-all-start = ((f32[32,16,256]{2,1,0:T(8,128)}), f32[32,16,256]{2,1,0:T(8,128)S(1)}, u32[]{:S(2)}, u32[]{:S(2)}) async-start(f32[32,16,256]{2,1,0:T(8,128)} %bitcast.122), calls=%async_computation | async-start | bytes 1048576 | tf_op jit(solution)/shard_map/all_to_all | solution.py:111
  18.1 16.6 %all-to-all-done = f32[32,16,256]{2,1,0:T(8,128)S(1)} async-done(((f32[32,16,256]{2,1,0:T(8,128)}), f32[32,16,256]{2,1,0:T(8,128)S(1)}, u32[]{:S(2)}, u32[]{:S(2)}) %all-to-all-start) | async-done | bytes 524320 | tf_op jit(solution)/shard_map/all_to_all | solution.py:111
  38.8 72.7 %psum.7 = f32[2,512]{1,0:T(2,128)S(1)} all-reduce(f32[2,512]{1,0:T(2,128)S(1)} %broadcast_select_fusion.1), channel_id=1, replica_groups=mesh['row'=32,'col'=8] {'row'}, use_global_device_ids=true, to_apply=%region_2.3 | all-reduce | flops 1024 | bytes 8192 | tf_op jit(solution)/shard_map/psum | solution.py:107
  120.0 3.9 exponential_multiply_fusion.2
  128.0 14.9 %shard_map.46 = (f32[128,128]{1,0:T(8,128)}, f32[128,128]{1,0:T(8,128)}) custom-call(f32[128,128]{1,0:T(8,128)} %slice.147.a_ref), custom_call_target="tpu_custom_call" | custom-call | tf_op jit(solution)/shard_map/pallas_call | solution.py:68
  145.7 14.4 %shard_map.47 = (f32[128,128]{1,0:T(8,128)}, f32[128,128]{1,0:T(8,128)}) custom-call(f32[128,128]{1,0:T(8,128)} %convolution_subtract_fusion.6.a_ref), custom_call_target="tpu_custom_call" | custom-call | tf_op jit(solution)/shard_map/pallas_call | solution.py:68
  166.1 14.4 %shard_map.48 = (f32[128,128]{1,0:T(8,128)}, f32[128,128]{1,0:T(8,128)}) custom-call(f32[128,128]{1,0:T(8,128)} %slice.152.a_ref), custom_call_target="tpu_custom_call" | custom-call | tf_op jit(solution)/shard_map/pallas_call | solution.py:68
  182.7 14.4 %shard_map.49 = (f32[128,128]{1,0:T(8,128)}, f32[128,128]{1,0:T(8,128)}) custom-call(f32[128,128]{1,0:T(8,128)} %convolution_subtract_fusion.5.a_ref), custom_call_target="tpu_custom_call" | custom-call | tf_op jit(solution)/shard_map/pallas_call | solution.py:68
  209.1 10.9 %exponential_multiply_fusion = f32[2560,1024]{1,0:T(8,128)S(1)} fusion(f32[2560,256]{1,0:T(8,128)} %bitcast_multiply_fusion, f32[1024]{0:T(1024)S(1)} %copy-done.39, f32[2560]{0:T(1024)S(1)} %add.161, f32[512,256]{1,0:T(8,128)S(1)} %copy-done.15, f32[512,256]{1,0:T(8,128)S(1)} %get-tuple-element.49), kind=kOutput, calls=%fused_computation.1 | convolution fusion | flops 4047765504 | bytes 14170112 | tf_op jit(solution)/shard_map/dot_general | solution.py:12
  220.0 5.8 %fusion.111 = (f32[5,512,512]{2,1,0:T(8,128)}, f32[5,512,512]{2,1,0:T(8,128)}) fusion(f32[5,512,1024]{2,1,0:T(8,128)S(1)} %bitcast.119), kind=kLoop, calls=%fused_computation.175 | loop fusion | bytes 20971520 | tf_op jit(solution)/shard_map/slice | solution.py:137
  225.7 6.1 %copy.65 = f32[5,512,512]{1,2,0:T(8,128)} copy(f32[5,512,512]{2,1,0:T(8,128)} %get-tuple-element.42) | data formatting | bytes 10485760
  231.9 5.7 %select_add_fusion = f32[5,512,512]{1,2,0:T(8,128)} fusion(f32[5,512,512]{1,2,0:T(8,128)} %copy.65, f32[512,512]{0,1:T(8,128)S(1)} %copy-done.8, pred[5]{0:T(512)(128)(4,1)S(1)} %get-tuple-element.55, pred[5]{0:T(512)(128)(4,1)S(1)} %copy-done.41), kind=kLoop, calls=%fused_computation.15 | loop fusion | flops 3932160 | bytes 11534346 | tf_op jit(solution)/shard_map/add | solution.py:136
  237.7 6.0 %copy.40 = f32[5,512,512]{2,1,0:T(8,128)} copy(f32[5,512,512]{1,2,0:T(8,128)} %select_add_fusion) | data formatting | bytes 10485760 | tf_op jit(solution)/shard_map/add | solution.py:136
  243.7 12.6 %fusion.4 = f32[3072,512]{1,0:T(8,128)S(1)} fusion(f32[2560,512]{1,0:T(8,128)} %bitcast.117, f32[512,512]{1,0:T(8,128)S(1)} %copy-done.6, f32[256,256]{1,0:T(8,128)S(1)} %copy-done.18, f32[128,128]{1,0:T(8,128)S(1)} %copy-done.26, f32[128,128]{1,0:T(8,128)S(1)} %copy-done.28, f32[128,256]{1,0:T(8,128)S(1)} %concatenate.193, f32[256,256]{1,0:T(8,128)S(1)} %copy-done.19), kind=kOutput, calls=%fused_computation.6 | convolution fusion | flops 9666822144 | bytes 13369344 | tf_op jit(solution)/shard_map/dot_general | solution.py:12
  256.3 2.6 copy-done.1
  258.9 3.1 convolution_subtract_fusion
  262.7 14.4 %shard_map.50 = (f32[128,128]{1,0:T(8,128)}, f32[128,128]{1,0:T(8,128)}) custom-call(f32[128,128]{1,0:T(8,128)} %slice.160.a_ref), custom_call_target="tpu_custom_call" | custom-call | tf_op jit(solution)/shard_map/pallas_call | solution.py:68
  279.2 14.4 %shard_map.51 = (f32[128,128]{1,0:T(8,128)}, f32[128,128]{1,0:T(8,128)}) custom-call(f32[128,128]{1,0:T(8,128)} %convolution_subtract_fusion.4.a_ref), custom_call_target="tpu_custom_call" | custom-call | tf_op jit(solution)/shard_map/pallas_call | solution.py:68
  299.5 14.4 %shard_map.52 = (f32[128,128]{1,0:T(8,128)}, f32[128,128]{1,0:T(8,128)}) custom-call(f32[128,128]{1,0:T(8,128)} %slice.165.a_ref), custom_call_target="tpu_custom_call" | custom-call | tf_op jit(solution)/shard_map/pallas_call | solution.py:68
  318.7 14.6 %shard_map.53 = (f32[128,128]{1,0:T(8,128)}, f32[128,128]{1,0:T(8,128)}) custom-call(f32[128,128]{1,0:T(8,128)} %convolution_subtract_fusion.3.a_ref), custom_call_target="tpu_custom_call" | custom-call | tf_op jit(solution)/shard_map/pallas_call | solution.py:68
  340.2 5.6 %bitcast_select_fusion = (f32[2560,512]{1,0:T(8,128)S(1)}, f32[2560,512]{1,0:T(8,128)}) fusion(f32[512,512]{1,0:T(8,128)S(1)} %fusion.38, pred[2560]{0:T(1024)(128)(4,1)S(1)} %broadcast_in_dim.224, f32[3072,512]{1,0:T(8,128)} %copy-done.1), kind=kLoop, calls=%fused_computation.10 | loop fusion | flops 1310720 | bytes 16779776 | tf_op jit(solution)/shard_map/jit(_where)/select_n | solution.py:145
  345.7 12.2 %fusion.55 = f32[5,512,512]{1,2,0:T(8,128)} fusion(f32[5,512,512]{2,1,0:T(8,128)S(1)} %bitcast.118, f32[3072,512]{1,0:T(8,128)} %copy-done.1), kind=kOutput, calls=%fused_computation.93 | convolution fusion | flops 8053063680 | bytes 11534336 | tf_op jit(solution)/shard_map/dot_general | solution.py:12
  358.0 6.1 %copy.64 = f32[5,512,512]{1,2,0:T(8,128)} copy(f32[5,512,512]{2,1,0:T(8,128)} %get-tuple-element.41) | data formatting | bytes 10485760
  364.1 13.7 %select_select_fusion = f32[5,512,512]{1,2,0:T(8,128)S(1)} fusion(f32[5,512,512]{1,2,0:T(8,128)} %fusion.55, f32[5,512,512]{1,2,0:T(8,128)} %copy.64, f32[512,512]{0,1:T(8,128)S(1)} %copy-done.22, f32[512,512]{0,1:T(8,128)S(1)} %copy-done.21, pred[5]{0:T(512)(128)(4,1)S(1)} %copy-done.46, pred[5]{0:T(512)(128)(4,1)S(1)} %copy-done.45, ...), kind=kOutput, calls=%fused_computation.11 | convolution fusion | flops 8063811584 | bytes 18612244 | tf_op jit(solution)/shard_map/dot_general | solution.py:12
  377.8 2.3 copy-done.4
  381.1 6.0 %copy.50 = f32[5,512,512]{1,2,0:T(8,128)} copy(f32[5,512,512]{2,1,0:T(8,128)} %bitcast.116) | data formatting | bytes 10485760 | tf_op jit(solution)/shard_map/reshape | solution.py:144
  387.1 3.3 broadcast_select_fusion
  390.5 2.4 copy-done.2
  393.9 2.5 copy.49
  396.4 2.5 copy.51
  399.5 5.9 %exponential_multiply_fusion.1 = f32[512,2048]{1,0:T(8,128)} fusion(f32[2048,256]{1,0:T(8,128)S(1)} %bitcast.121, f32[2048]{0:T(1024)S(1)} %bitcast.129, f32[512]{0:T(512)S(1)} %copy-done.40, f32[512,256]{1,0:T(8,128)S(1)} %copy-done.5, f32[256]{0:T(256)S(1)} %copy-done.36), kind=kOutput, calls=%fused_computation.26 | convolution fusion | flops 1619132416 | bytes 6827008 | tf_op jit(solution)/shard_map/dot_general | solution.py:12
  405.5 11.7 %fusion.19 = f32[1,4,1,512,512]{4,3,2,1,0:T(8,128)} fusion(f32[64,4,8,512]{3,2,1,0:T(8,128)} %bitcast.130, f32[512,512]{1,0:T(8,128)S(1)} %copy-done.20, f32[512,512]{1,0:T(8,128)} %copy.51, f32[512,512]{1,0:T(8,128)S(1)} %copy-done.23, pred[4]{0:T(512)(128)(4,1)S(1)} %copy-done.42, pred[4]{0:T(512)(128)(4,1)S(1)} %copy-done.48, ...), kind=kOutput, calls=%fused_computation.25 | convolution fusion | flops 6452412416 | bytes 22020116 | tf_op jit(solution)/shard_map/dot_general | solution.py:12
  (185 shorter events, 62.2 us)
Async XLA Ops:
  6.5 109.2 %copy-start.5 = (f32[512,256]{1,0:T(8,128)S(1)}, f32[512,256]{1,0:T(8,128)}, u32[]{:S(2)}) copy-start(f32[512,256]{1,0:T(8,128)} %param.4) | copy-start | bytes 1572868
  6.5 106.4 %copy-start = (s32[32]{0:T(128)S(1)}, s32[32]{0:T(128)}, u32[]{:S(2)}) copy-start(s32[32]{0:T(128)} %param.7) | copy-start | bytes 388
  6.5 109.9 %copy-start.37 = (f32[512]{0:T(512)S(1)}, f32[512]{0:T(512)}, u32[]{:S(2)}) copy-start(f32[512]{0:T(512)} %param.5) | copy-start | bytes 6148
  6.5 109.2 %copy-start.36 = (f32[256]{0:T(256)S(1)}, f32[256]{0:T(256)}, u32[]{:S(2)}) copy-start(f32[256]{0:T(256)} %param.6) | copy-start | bytes 3076
  6.5 28.2 %all-to-all-start = ((f32[32,16,256]{2,1,0:T(8,128)}), f32[32,16,256]{2,1,0:T(8,128)S(1)}, u32[]{:S(2)}, u32[]{:S(2)}) async-start(f32[32,16,256]{2,1,0:T(8,128)} %bitcast.122), calls=%async_computation | async-start | bytes 1048576 | tf_op jit(solution)/shard_map/all_to_all | solution.py:111
  18.0 100.3 %all-gather.4.cloned.1.call-start = ((), (), s32[]{:S(2)}) async-start(), calls=%async_computation.1 | async-start | bytes 1081344 | tf_op jit(solution)/shard_map/all_gather | solution.py:112
  35.3 170.0 %all-gather.6.cloned.1.call-start = ((), (), s32[]{:S(2)}) async-start(), calls=%async_computation.2 | async-start | bytes 2162688 | tf_op jit(solution)/shard_map/all_gather | solution.py:116
  127.3 34.0 %copy-start.11 = (f32[512,512]{1,0:T(8,128)}, f32[512,512]{1,0:T(8,128)S(1)}, u32[]{:S(2)}) copy-start(f32[512,512]{1,0:T(8,128)S(1)} %get-tuple-element.45) | copy-start | bytes 3145732
  142.9 56.5 %copy-start.16 = (f32[128,128]{1,0:T(8,128)S(1)}, f32[128,128]{1,0:T(8,128)}, u32[]{:S(2)}) copy-start(f32[128,128]{1,0:T(8,128)} %get-tuple-element.22) | copy-start | bytes 196612
  160.1 39.2 %copy-start.24 = (f32[128,128]{1,0:T(8,128)S(1)}, f32[128,128]{1,0:T(8,128)}, u32[]{:S(2)}) copy-start(f32[128,128]{1,0:T(8,128)} %get-tuple-element.24) | copy-start | bytes 196612
  162.3 37.0 %copy-start.30 = (f32[128,128]{1,0:T(8,128)S(1)}, f32[128,128]{1,0:T(8,128)}, u32[]{:S(2)}) copy-start(f32[128,128]{1,0:T(8,128)} %copy.32) | copy-start | bytes 196612
  180.5 23.1 %copy-start.29 = (f32[128,128]{1,0:T(8,128)S(1)}, f32[128,128]{1,0:T(8,128)}, u32[]{:S(2)}) copy-start(f32[128,128]{1,0:T(8,128)} %get-tuple-element.26) | copy-start | bytes 196612
  197.1 6.2 %copy-start.26 = (f32[128,128]{1,0:T(8,128)S(1)}, f32[128,128]{1,0:T(8,128)}, u32[]{:S(2)}) copy-start(f32[128,128]{1,0:T(8,128)} %get-tuple-element.28) | copy-start | bytes 196612
  225.7 6.2 %copy-start.8 = (f32[512,512]{0,1:T(8,128)S(1)}, f32[512,512]{0,1:T(8,128)}, u32[]{:S(2)}) copy-start(f32[512,512]{0,1:T(8,128)} %copy.39) | copy-start | bytes 3145732
  225.7 6.2 %copy-start.41 = (pred[5]{0:T(512)(128)(4,1)S(1)}, pred[5]{0:T(512)(128)(4,1)}, u32[]{:S(2)}) copy-start(pred[5]{0:T(512)(128)(4,1)} %get-tuple-element.58) | copy-start | bytes 19
  262.0 32.8 %copy-start.12 = (f32[512,512]{1,0:T(8,128)}, f32[512,512]{1,0:T(8,128)S(1)}, u32[]{:S(2)}) copy-start(f32[512,512]{1,0:T(8,128)S(1)} %convolution_subtract_fusion) | copy-start | bytes 3145732
  277.2 59.6 %copy-start.17 = (f32[128,128]{1,0:T(8,128)S(1)}, f32[128,128]{1,0:T(8,128)}, u32[]{:S(2)}) copy-start(f32[128,128]{1,0:T(8,128)} %get-tuple-element.29) | copy-start | bytes 196612
  277.2 60.7 %copy-start.34 = (f32[128,128]{1,0:T(8,128)S(1)}, f32[128,128]{1,0:T(8,128)}, u32[]{:S(2)}) copy-start(f32[128,128]{1,0:T(8,128)} %get-tuple-element.33) | copy-start | bytes 196612
  293.7 43.1 %copy-start.25 = (f32[128,128]{1,0:T(8,128)S(1)}, f32[128,128]{1,0:T(8,128)}, u32[]{:S(2)}) copy-start(f32[128,128]{1,0:T(8,128)} %get-tuple-element.30) | copy-start | bytes 196612
  295.9 42.0 %copy-start.35 = (f32[128,128]{1,0:T(8,128)S(1)}, f32[128,128]{1,0:T(8,128)}, u32[]{:S(2)}) copy-start(f32[128,128]{1,0:T(8,128)} %get-tuple-element.34) | copy-start | bytes 196612
  313.9 24.0 %copy-start.33 = (f32[128,128]{1,0:T(8,128)S(1)}, f32[128,128]{1,0:T(8,128)}, u32[]{:S(2)}) copy-start(f32[128,128]{1,0:T(8,128)} %get-tuple-element.35) | copy-start | bytes 196612
  357.9 6.1 %copy-start.22 = (f32[512,512]{0,1:T(8,128)S(1)}, f32[512,512]{0,1:T(8,128)}, u32[]{:S(2)}) copy-start(f32[512,512]{0,1:T(8,128)} %copy.48) | copy-start | bytes 3145732
  357.9 6.1 %copy-start.31 = (f32[128,128]{1,0:T(8,128)S(1)}, f32[128,128]{1,0:T(8,128)}, u32[]{:S(2)}) copy-start(f32[128,128]{1,0:T(8,128)} %get-tuple-element.32) | copy-start | bytes 196612
  357.9 6.1 %copy-start.32 = (f32[256,256]{1,0:T(8,128)S(1)}, f32[256,256]{1,0:T(8,128)}, u32[]{:S(2)}) copy-start(f32[256,256]{1,0:T(8,128)} %select_maximum_fusion.6) | copy-start | bytes 786436
  357.9 6.1 %copy-start.44 = (pred[5]{0:T(512)(128)(4,1)S(1)}, pred[5]{0:T(512)(128)(4,1)}, u32[]{:S(2)}) copy-start(pred[5]{0:T(512)(128)(4,1)} %get-tuple-element.54) | copy-start | bytes 19
  357.9 6.1 %copy-start.45 = (pred[5]{0:T(512)(128)(4,1)S(1)}, pred[5]{0:T(512)(128)(4,1)}, u32[]{:S(2)}) copy-start(pred[5]{0:T(512)(128)(4,1)} %get-tuple-element.56) | copy-start | bytes 19
  357.9 6.1 %copy-start.46 = (pred[5]{0:T(512)(128)(4,1)S(1)}, pred[5]{0:T(512)(128)(4,1)}, u32[]{:S(2)}) copy-start(pred[5]{0:T(512)(128)(4,1)} %get-tuple-element.57) | copy-start | bytes 19
  357.9 6.1 %copy-start.47 = (pred[5]{0:T(512)(128)(4,1)S(1)}, pred[5]{0:T(512)(128)(4,1)}, u32[]{:S(2)}) copy-start(pred[5]{0:T(512)(128)(4,1)} %get-tuple-element.39) | copy-start | bytes 19
  392.9 6.1 %copy-start.3 = (f32[4,1,512,256]{3,2,1,0:T(8,128)S(1)}, f32[4,1,512,256]{3,2,1,0:T(8,128)}, u32[]{:S(2)}) copy-start(f32[4,1,512,256]{3,2,1,0:T(8,128)} %all-gather.6.cloned.1.call-done) | copy-start | bytes 6291460
  392.9 6.5 %copy-start.40 = (f32[512]{0:T(512)S(1)}, f32[512]{0:T(512)}, u32[]{:S(2)}) copy-start(f32[512]{0:T(512)} %fusion.67) | copy-start | bytes 6148
  399.0 6.4 %copy-start.20 = (f32[512,512]{1,0:T(8,128)S(1)}, f32[512,512]{1,0:T(8,128)}, u32[]{:S(2)}) copy-start(f32[512,512]{1,0:T(8,128)} %fusion.57) | copy-start | bytes 3145732
  399.0 6.4 %copy-start.23 = (f32[512,512]{1,0:T(8,128)S(1)}, f32[512,512]{1,0:T(8,128)}, u32[]{:S(2)}) copy-start(f32[512,512]{1,0:T(8,128)} %copy.49) | copy-start | bytes 3145732
  (24 other events, 120.8 us)
Sparse Core Ops, SparseCore 0:
  35.5 73.6 all-gather.3
  118.4 72.0 all-gather.5

commit v5 on v4

--- a/solution.py
+++ b/solution.py
@@ -25,7 +25,7 @@
 
 
 BASE = 128
-PHASE = 32
+PHASE = 16
 
 
 def _chol_base_kernel(a_ref, l_ref, m_ref, w_ref):
@@ -109,7 +109,7 @@
 
     chunks = points.reshape(n_row, piece, points.shape[1])
     recv = lax.all_to_all(chunks, "row", 0, 0, tiled=True)
-    tiles01 = lax.all_gather(recv[:2], "row", axis=1, tiled=True)
+    tiles01 = lax.all_gather(recv[:2] + 0.0 * nug[0, 0], "row", axis=1, tiled=True)
     mine = lax.dynamic_slice_in_dim(
         recv.reshape(blocks, n_col, piece, points.shape[1]), my_col, 1, axis=1
     )[:, 0]

time: 431 us -> 481 us (1.12)
  waiting for transfers between devices: 16.6 us -> 60.7 us
  blocking collectives: 72.7 us -> 78.3 us
    all_gather x1, waiting for transfers between devices: 0.02 us -> 60.7 us  [body(): lax.all_gather(recv[:2] + 0.0 * nug[0, 0], 'row', axis=1, tiled=True)]
    all_to_all x1, waiting for transfers between devices: 16.6 us -> 0.01 us  [body(): recv = lax.all_to_all(chunks, 'row', 0, 0, tiled=True)]
    psum x1, blocking collectives: 72.7 us -> 78.3 us  [body(): nug = lax.psum(jnp.where(slot, nugget[None, :], 0.0), 'row')]
  transfers between devices with their start and end apart: 3 -> 3, of which waited for: 1 -> 1; matrix products, arithmetic and copies ran while one was open for 9% -> 8% of each run, Pallas kernels for 14% -> 12%
where the time goes in v5:
time: 481 us; the launch traced here: 475 us
  Pallas kernels  115 us (24%)
  matrix products  98.9 us (21%)
  blocking collectives  78.3 us (16%)
  local copies, waits for them, and re-layouts  62 us (13%)
  waiting for transfers between devices  60.7 us (13%)
  other arithmetic  32.5 us (7%)
  between operations  15.3 us (3%)
  starting transfers between devices  11.5 us (2%)
    pallas_call x8, Pallas kernels, chol_base(): pl.pallas_call(_chol_base_kernel, out_shape=(jax.ShapeDtypeStruct((n, n),...  115 us
    dot_general x20, matrix products, mm(): lax.dot_general(a, b, (((1,), (1,)), ((), ())), precision=precision, pref...  88 us
    psum x1, blocking collectives, body(): nug = lax.psum(jnp.where(slot, nugget[None, :], 0.0), 'row')  78.3 us
    all_gather x1, waiting for transfers between devices, body(): lax.all_gather(recv[:2] + 0.0 * nug[0, 0], 'row', axis=1, tiled=True)  60.7 us
    unnamed x105, local copies, waits for them, and re-layouts  21.8 us
    all_to_all x1, starting transfers between devices, body(): recv = lax.all_to_all(chunks, 'row', 0, 0, tiled=True)  11.4 us
    dot_general x12, matrix products, dot(): return jnp.dot(a, b, precision=HI, preferred_element_type=jnp.float32)  10.9 us
  transfers between devices with their start and end apart: 3, of which 1 were waited for; matrix products, arithmetic and copies ran while one was open for 8% of the time, Pallas kernels for 12%

profile of v5, /device:TPU:8, one launch (start us, length us, event | category | flops | bytes accessed | tf_op | source)
XLA Modules:
  0.0 474.6 jit_solution(3977701432531984686)
XLA Ops:
  6.5 11.4 %all-to-all-start = ((f32[32,16,256]{2,1,0:T(8,128)}), f32[32,16,256]{2,1,0:T(8,128)S(1)}, u32[]{:S(2)}, u32[]{:S(2)}) async-start(f32[32,16,256]{2,1,0:T(8,128)} %bitcast.123), calls=%async_computation | async-start | bytes 1048576 | tf_op jit(solution)/shard_map/all_to_all | solution.py:111
  18.8 78.3 %psum.7 = f32[2,512]{1,0:T(2,128)S(1)} all-reduce(f32[2,512]{1,0:T(2,128)S(1)} %broadcast_select_fusion.1), channel_id=1, replica_groups=mesh['row'=32,'col'=8] {'row'}, use_global_device_ids=true, to_apply=%region_1.2 | all-reduce | flops 1024 | bytes 8192 | tf_op jit(solution)/shard_map/psum | solution.py:107
  108.5 60.7 %all-gather.4.cloned.1.call-done = f32[2,512,256]{2,1,0:T(8,128)} async-done(((f32[2,16,256]{2,1,0:T(8,128)}), f32[2,512,256]{2,1,0:T(8,128)}) %all-gather.4.cloned.1.call-update) | async-done | bytes 1048592 | tf_op jit(solution)/shard_map/all_gather | solution.py:112
  170.8 3.9 exponential_multiply_fusion.2
  178.8 14.8 %shard_map.46 = (f32[128,128]{1,0:T(8,128)}, f32[128,128]{1,0:T(8,128)}) custom-call(f32[128,128]{1,0:T(8,128)} %slice.152.a_ref), custom_call_target="tpu_custom_call" | custom-call | tf_op jit(solution)/shard_map/pallas_call | solution.py:68
  196.4 14.3 %shard_map.47 = (f32[128,128]{1,0:T(8,128)}, f32[128,128]{1,0:T(8,128)}) custom-call(f32[128,128]{1,0:T(8,128)} %convolution_subtract_fusion.6.a_ref), custom_call_target="tpu_custom_call" | custom-call | tf_op jit(solution)/shard_map/pallas_call | solution.py:68
  216.7 14.3 %shard_map.48 = (f32[128,128]{1,0:T(8,128)}, f32[128,128]{1,0:T(8,128)}) custom-call(f32[128,128]{1,0:T(8,128)} %slice.157.a_ref), custom_call_target="tpu_custom_call" | custom-call | tf_op jit(solution)/shard_map/pallas_call | solution.py:68
  233.2 14.3 %shard_map.49 = (f32[128,128]{1,0:T(8,128)}, f32[128,128]{1,0:T(8,128)}) custom-call(f32[128,128]{1,0:T(8,128)} %convolution_subtract_fusion.5.a_ref), custom_call_target="tpu_custom_call" | custom-call | tf_op jit(solution)/shard_map/pallas_call | solution.py:68
  259.6 10.9 %exponential_multiply_fusion = f32[2560,1024]{1,0:T(8,128)S(1)} fusion(f32[2560,256]{1,0:T(8,128)} %bitcast_multiply_fusion, f32[1024]{0:T(1024)S(1)} %copy-done.39, f32[2560]{0:T(1024)S(1)} %add.167, f32[512,256]{1,0:T(8,128)S(1)} %copy-done.15, f32[512,256]{1,0:T(8,128)S(1)} %get-tuple-element.49), kind=kOutput, calls=%fused_computation.1 | convolution fusion | flops 4047765504 | bytes 14170112 | tf_op jit(solution)/shard_map/dot_general | solution.py:12
  270.4 5.8 %fusion.111 = (f32[5,512,512]{2,1,0:T(8,128)}, f32[5,512,512]{2,1,0:T(8,128)}) fusion(f32[5,512,1024]{2,1,0:T(8,128)S(1)} %bitcast.120), kind=kLoop, calls=%fused_computation.176 | loop fusion | bytes 20971520 | tf_op jit(solution)/shard_map/slice | solution.py:137
  276.2 6.1 %copy.65 = f32[5,512,512]{1,2,0:T(8,128)} copy(f32[5,512,512]{2,1,0:T(8,128)} %get-tuple-element.42) | data formatting | bytes 10485760
  282.3 5.7 %select_add_fusion = f32[5,512,512]{1,2,0:T(8,128)} fusion(f32[5,512,512]{1,2,0:T(8,128)} %copy.65, f32[512,512]{0,1:T(8,128)S(1)} %copy-done.8, pred[5]{0:T(512)(128)(4,1)S(1)} %get-tuple-element.55, pred[5]{0:T(512)(128)(4,1)S(1)} %copy-done.41), kind=kLoop, calls=%fused_computation.15 | loop fusion | flops 3932160 | bytes 11534346 | tf_op jit(solution)/shard_map/add | solution.py:136
  288.1 6.0 %copy.40 = f32[5,512,512]{2,1,0:T(8,128)} copy(f32[5,512,512]{1,2,0:T(8,128)} %select_add_fusion) | data formatting | bytes 10485760 | tf_op jit(solution)/shard_map/add | solution.py:136
  294.1 12.6 %fusion.4 = f32[3072,512]{1,0:T(8,128)S(1)} fusion(f32[2560,512]{1,0:T(8,128)} %bitcast.118, f32[512,512]{1,0:T(8,128)S(1)} %copy-done.6, f32[256,256]{1,0:T(8,128)S(1)} %copy-done.18, f32[128,128]{1,0:T(8,128)S(1)} %copy-done.26, f32[128,128]{1,0:T(8,128)S(1)} %copy-done.28, f32[128,256]{1,0:T(8,128)S(1)} %concatenate.193, f32[256,256]{1,0:T(8,128)S(1)} %copy-done.19), kind=kOutput, calls=%fused_computation.6 | convolution fusion | flops 9666822144 | bytes 13369344 | tf_op jit(solution)/shard_map/dot_general | solution.py:12
  306.7 2.6 copy-done.1
  309.4 3.1 convolution_subtract_fusion
  313.2 14.3 %shard_map.50 = (f32[128,128]{1,0:T(8,128)}, f32[128,128]{1,0:T(8,128)}) custom-call(f32[128,128]{1,0:T(8,128)} %slice.165.a_ref), custom_call_target="tpu_custom_call" | custom-call | tf_op jit(solution)/shard_map/pallas_call | solution.py:68
  329.6 14.3 %shard_map.51 = (f32[128,128]{1,0:T(8,128)}, f32[128,128]{1,0:T(8,128)}) custom-call(f32[128,128]{1,0:T(8,128)} %convolution_subtract_fusion.4.a_ref), custom_call_target="tpu_custom_call" | custom-call | tf_op jit(solution)/shard_map/pallas_call | solution.py:68
  349.7 14.3 %shard_map.52 = (f32[128,128]{1,0:T(8,128)}, f32[128,128]{1,0:T(8,128)}) custom-call(f32[128,128]{1,0:T(8,128)} %slice.170.a_ref), custom_call_target="tpu_custom_call" | custom-call | tf_op jit(solution)/shard_map/pallas_call | solution.py:68
  368.9 14.5 %shard_map.53 = (f32[128,128]{1,0:T(8,128)}, f32[128,128]{1,0:T(8,128)}) custom-call(f32[128,128]{1,0:T(8,128)} %convolution_subtract_fusion.3.a_ref), custom_call_target="tpu_custom_call" | custom-call | tf_op jit(solution)/shard_map/pallas_call | solution.py:68
  390.2 5.6 %bitcast_select_fusion = (f32[2560,512]{1,0:T(8,128)S(1)}, f32[2560,512]{1,0:T(8,128)}) fusion(f32[512,512]{1,0:T(8,128)S(1)} %fusion.38, pred[2560]{0:T(1024)(128)(4,1)S(1)} %broadcast_in_dim.224, f32[3072,512]{1,0:T(8,128)} %copy-done.1), kind=kLoop, calls=%fused_computation.10 | loop fusion | flops 1310720 | bytes 16779776 | tf_op jit(solution)/shard_map/jit(_where)/select_n | solution.py:145
  395.8 12.2 %fusion.55 = f32[5,512,512]{1,2,0:T(8,128)} fusion(f32[5,512,512]{2,1,0:T(8,128)S(1)} %bitcast.119, f32[3072,512]{1,0:T(8,128)} %copy-done.1), kind=kOutput, calls=%fused_computation.93 | convolution fusion | flops 8053063680 | bytes 11534336 | tf_op jit(solution)/shard_map/dot_general | solution.py:12
  408.0 6.1 %copy.64 = f32[5,512,512]{1,2,0:T(8,128)} copy(f32[5,512,512]{2,1,0:T(8,128)} %get-tuple-element.41) | data formatting | bytes 10485760
  414.1 13.7 %select_select_fusion = f32[5,512,512]{1,2,0:T(8,128)S(1)} fusion(f32[5,512,512]{1,2,0:T(8,128)} %fusion.55, f32[5,512,512]{1,2,0:T(8,128)} %copy.64, f32[512,512]{0,1:T(8,128)S(1)} %copy-done.22, f32[512,512]{0,1:T(8,128)S(1)} %copy-done.21, pred[5]{0:T(512)(128)(4,1)S(1)} %copy-done.46, pred[5]{0:T(512)(128)(4,1)S(1)} %copy-done.45, ...), kind=kOutput, calls=%fused_computation.11 | convolution fusion | flops 8063811584 | bytes 18612244 | tf_op jit(solution)/shard_map/dot_general | solution.py:12
  427.8 2.3 copy-done.4
  431.2 6.0 %copy.50 = f32[5,512,512]{1,2,0:T(8,128)} copy(f32[5,512,512]{2,1,0:T(8,128)} %bitcast.117) | data formatting | bytes 10485760 | tf_op jit(solution)/shard_map/reshape | solution.py:144
  437.2 3.3 broadcast_select_fusion
  440.5 2.4 copy-done.2
  444.0 2.5 copy.49
  446.5 2.5 copy.51
  449.5 5.9 %exponential_multiply_fusion.1 = f32[512,2048]{1,0:T(8,128)} fusion(f32[2048,256]{1,0:T(8,128)S(1)} %bitcast.122, f32[2048]{0:T(1024)S(1)} %bitcast.130, f32[512]{0:T(512)S(1)} %copy-done.40, f32[512,256]{1,0:T(8,128)S(1)} %copy-done.5, f32[256]{0:T(256)S(1)} %copy-done.36), kind=kOutput, calls=%fused_computation.26 | convolution fusion | flops 1619132416 | bytes 6827008 | tf_op jit(solution)/shard_map/dot_general | solution.py:12
  455.5 11.7 %fusion.19 = f32[1,4,1,512,512]{4,3,2,1,0:T(8,128)} fusion(f32[64,4,8,512]{3,2,1,0:T(8,128)} %bitcast.131, f32[512,512]{1,0:T(8,128)S(1)} %copy-done.20, f32[512,512]{1,0:T(8,128)} %copy.51, f32[512,512]{1,0:T(8,128)S(1)} %copy-done.23, pred[4]{0:T(512)(128)(4,1)S(1)} %copy-done.42, pred[4]{0:T(512)(128)(4,1)S(1)} %copy-done.48, ...), kind=kOutput, calls=%fused_computation.25 | convolution fusion | flops 6452412416 | bytes 22020116 | tf_op jit(solution)/shard_map/dot_general | solution.py:12
  (186 shorter events, 62.7 us)
Async XLA Ops:
  6.5 99.4 %copy-start.5 = (f32[512,256]{1,0:T(8,128)S(1)}, f32[512,256]{1,0:T(8,128)}, u32[]{:S(2)}) copy-start(f32[512,256]{1,0:T(8,128)} %param.4) | copy-start | bytes 1572868
  6.5 100.1 %copy-start.37 = (f32[512]{0:T(512)S(1)}, f32[512]{0:T(512)}, u32[]{:S(2)}) copy-start(f32[512]{0:T(512)} %param.5) | copy-start | bytes 6148
  6.5 96.6 %copy-start = (s32[32]{0:T(128)S(1)}, s32[32]{0:T(128)}, u32[]{:S(2)}) copy-start(s32[32]{0:T(128)} %param.7) | copy-start | bytes 388
  6.5 99.4 %copy-start.36 = (f32[256]{0:T(256)S(1)}, f32[256]{0:T(256)}, u32[]{:S(2)}) copy-start(f32[256]{0:T(256)} %param.6) | copy-start | bytes 3076
  6.5 91.7 %all-to-all-start = ((f32[32,16,256]{2,1,0:T(8,128)}), f32[32,16,256]{2,1,0:T(8,128)S(1)}, u32[]{:S(2)}, u32[]{:S(2)}) async-start(f32[32,16,256]{2,1,0:T(8,128)} %bitcast.123), calls=%async_computation | async-start | bytes 1048576 | tf_op jit(solution)/shard_map/all_to_all | solution.py:111
  18.0 151.1 %all-gather.4.cloned.1.call-start = ((), (), s32[]{:S(2)}) async-start(), calls=%async_computation.1 | async-start | bytes 1081344 | tf_op jit(solution)/shard_map/all_gather | solution.py:112
  98.9 156.8 %all-gather.6.cloned.1.call-start = ((), (), s32[]{:S(2)}) async-start(), calls=%async_computation.2 | async-start | bytes 2162688 | tf_op jit(solution)/shard_map/all_gather | solution.py:116
  178.1 33.8 %copy-start.11 = (f32[512,512]{1,0:T(8,128)}, f32[512,512]{1,0:T(8,128)S(1)}, u32[]{:S(2)}) copy-start(f32[512,512]{1,0:T(8,128)S(1)} %get-tuple-element.45) | copy-start | bytes 3145732
  193.6 56.2 %copy-start.16 = (f32[128,128]{1,0:T(8,128)S(1)}, f32[128,128]{1,0:T(8,128)}, u32[]{:S(2)}) copy-start(f32[128,128]{1,0:T(8,128)} %get-tuple-element.22) | copy-start | bytes 196612
  210.7 39.1 %copy-start.24 = (f32[128,128]{1,0:T(8,128)S(1)}, f32[128,128]{1,0:T(8,128)}, u32[]{:S(2)}) copy-start(f32[128,128]{1,0:T(8,128)} %get-tuple-element.24) | copy-start | bytes 196612
  213.0 36.8 %copy-start.30 = (f32[128,128]{1,0:T(8,128)S(1)}, f32[128,128]{1,0:T(8,128)}, u32[]{:S(2)}) copy-start(f32[128,128]{1,0:T(8,128)} %copy.32) | copy-start | bytes 196612
  231.0 23.0 %copy-start.29 = (f32[128,128]{1,0:T(8,128)S(1)}, f32[128,128]{1,0:T(8,128)}, u32[]{:S(2)}) copy-start(f32[128,128]{1,0:T(8,128)} %get-tuple-element.26) | copy-start | bytes 196612
  247.6 6.2 %copy-start.26 = (f32[128,128]{1,0:T(8,128)S(1)}, f32[128,128]{1,0:T(8,128)}, u32[]{:S(2)}) copy-start(f32[128,128]{1,0:T(8,128)} %get-tuple-element.28) | copy-start | bytes 196612
  276.2 6.1 %copy-start.8 = (f32[512,512]{0,1:T(8,128)S(1)}, f32[512,512]{0,1:T(8,128)}, u32[]{:S(2)}) copy-start(f32[512,512]{0,1:T(8,128)} %copy.39) | copy-start | bytes 3145732
  276.2 6.1 %copy-start.41 = (pred[5]{0:T(512)(128)(4,1)S(1)}, pred[5]{0:T(512)(128)(4,1)}, u32[]{:S(2)}) copy-start(pred[5]{0:T(512)(128)(4,1)} %get-tuple-element.58) | copy-start | bytes 19
  312.5 32.6 %copy-start.12 = (f32[512,512]{1,0:T(8,128)}, f32[512,512]{1,0:T(8,128)S(1)}, u32[]{:S(2)}) copy-start(f32[512,512]{1,0:T(8,128)S(1)} %convolution_subtract_fusion) | copy-start | bytes 3145732
  327.5 59.3 %copy-start.17 = (f32[128,128]{1,0:T(8,128)S(1)}, f32[128,128]{1,0:T(8,128)}, u32[]{:S(2)}) copy-start(f32[128,128]{1,0:T(8,128)} %get-tuple-element.29) | copy-start | bytes 196612
  327.5 60.4 %copy-start.34 = (f32[128,128]{1,0:T(8,128)S(1)}, f32[128,128]{1,0:T(8,128)}, u32[]{:S(2)}) copy-start(f32[128,128]{1,0:T(8,128)} %get-tuple-element.33) | copy-start | bytes 196612
  343.9 42.9 %copy-start.25 = (f32[128,128]{1,0:T(8,128)S(1)}, f32[128,128]{1,0:T(8,128)}, u32[]{:S(2)}) copy-start(f32[128,128]{1,0:T(8,128)} %get-tuple-element.30) | copy-start | bytes 196612
  346.1 41.8 %copy-start.35 = (f32[128,128]{1,0:T(8,128)S(1)}, f32[128,128]{1,0:T(8,128)}, u32[]{:S(2)}) copy-start(f32[128,128]{1,0:T(8,128)} %get-tuple-element.34) | copy-start | bytes 196612
  364.1 23.9 %copy-start.33 = (f32[128,128]{1,0:T(8,128)S(1)}, f32[128,128]{1,0:T(8,128)}, u32[]{:S(2)}) copy-start(f32[128,128]{1,0:T(8,128)} %get-tuple-element.35) | copy-start | bytes 196612
  408.0 6.1 %copy-start.22 = (f32[512,512]{0,1:T(8,128)S(1)}, f32[512,512]{0,1:T(8,128)}, u32[]{:S(2)}) copy-start(f32[512,512]{0,1:T(8,128)} %copy.48) | copy-start | bytes 3145732
  408.0 6.1 %copy-start.31 = (f32[128,128]{1,0:T(8,128)S(1)}, f32[128,128]{1,0:T(8,128)}, u32[]{:S(2)}) copy-start(f32[128,128]{1,0:T(8,128)} %get-tuple-element.32) | copy-start | bytes 196612
  408.0 6.1 %copy-start.32 = (f32[256,256]{1,0:T(8,128)S(1)}, f32[256,256]{1,0:T(8,128)}, u32[]{:S(2)}) copy-start(f32[256,256]{1,0:T(8,128)} %select_maximum_fusion.6) | copy-start | bytes 786436
  408.0 6.1 %copy-start.44 = (pred[5]{0:T(512)(128)(4,1)S(1)}, pred[5]{0:T(512)(128)(4,1)}, u32[]{:S(2)}) copy-start(pred[5]{0:T(512)(128)(4,1)} %get-tuple-element.54) | copy-start | bytes 19
  408.0 6.1 %copy-start.45 = (pred[5]{0:T(512)(128)(4,1)S(1)}, pred[5]{0:T(512)(128)(4,1)}, u32[]{:S(2)}) copy-start(pred[5]{0:T(512)(128)(4,1)} %get-tuple-element.56) | copy-start | bytes 19
  408.0 6.1 %copy-start.46 = (pred[5]{0:T(512)(128)(4,1)S(1)}, pred[5]{0:T(512)(128)(4,1)}, u32[]{:S(2)}) copy-start(pred[5]{0:T(512)(128)(4,1)} %get-tuple-element.57) | copy-start | bytes 19
  408.0 6.1 %copy-start.47 = (pred[5]{0:T(512)(128)(4,1)S(1)}, pred[5]{0:T(512)(128)(4,1)}, u32[]{:S(2)}) copy-start(pred[5]{0:T(512)(128)(4,1)} %get-tuple-element.39) | copy-start | bytes 19
  442.9 6.1 %copy-start.3 = (f32[4,1,512,256]{3,2,1,0:T(8,128)S(1)}, f32[4,1,512,256]{3,2,1,0:T(8,128)}, u32[]{:S(2)}) copy-start(f32[4,1,512,256]{3,2,1,0:T(8,128)} %all-gather.6.cloned.1.call-done) | copy-start | bytes 6291460
  442.9 6.5 %copy-start.40 = (f32[512]{0:T(512)S(1)}, f32[512]{0:T(512)}, u32[]{:S(2)}) copy-start(f32[512]{0:T(512)} %fusion.67) | copy-start | bytes 6148
  449.0 6.4 %copy-start.20 = (f32[512,512]{1,0:T(8,128)S(1)}, f32[512,512]{1,0:T(8,128)}, u32[]{:S(2)}) copy-start(f32[512,512]{1,0:T(8,128)} %fusion.57) | copy-start | bytes 3145732
  449.1 6.4 %copy-start.23 = (f32[512,512]{1,0:T(8,128)S(1)}, f32[512,512]{1,0:T(8,128)}, u32[]{:S(2)}) copy-start(f32[512,512]{1,0:T(8,128)} %copy.49) | copy-start | bytes 3145732
  (24 other events, 120.8 us)
Sparse Core Ops, SparseCore 0:
  99.0 70.0 all-gather.3
  171.7 75.8 all-gather.5

commit v6 on v3

--- a/solution.py
+++ b/solution.py
@@ -98,73 +98,65 @@
     n_row = lax.axis_size("row")
     n_col = lax.axis_size("col")
     blocks = n_row // n_col
-    tile = points.shape[0]
+    tile, cov = points.shape
     piece = tile // n_row
     my_row = lax.axis_index("row")
     my_col = lax.axis_index("col")
 
-    chunks = points.reshape(n_row, piece, points.shape[1])
-    recv = lax.all_to_all(chunks, "row", 0, 0, tiled=True)
-    mine = lax.dynamic_slice_in_dim(
-        recv.reshape(blocks, n_col, piece, points.shape[1]), my_col, 1, axis=1
-    )[:, 0]
+    flat = points.reshape(n_row, piece * cov)
+    nug_pad = jnp.pad(nugget.reshape(n_row, piece), ((0, 0), (0, 128 - piece)))
+    recv = lax.all_to_all(jnp.concatenate([flat, nug_pad], axis=1), "row", 0, 0, tiled=True)
+    width = recv.shape[1]
+    mine = lax.dynamic_slice_in_dim(recv.reshape(blocks, n_col, width), my_col, 1, axis=1)[:, 0]
     sel = jnp.concatenate([recv[:2], mine], axis=0)
-    tiles_x = lax.all_gather(sel, "row", axis=1, tiled=True)
-    slot = jnp.arange(2, dtype=jnp.int32)[:, None] == my_row
-    nug = lax.psum(jnp.where(slot, nugget[None, :], 0.0), "row")
-    x0, x1 = tiles_x[0], tiles_x[1]
-    xcols = tiles_x[2:]
-    n0, n1 = nug[0], nug[1]
+    got = lax.all_gather(sel, "row", axis=1)
+    xs = got[:, :, : piece * cov].reshape(2 + blocks, tile, cov)
+    ns = got[:, :, piece * cov : piece * cov + piece].reshape(2 + blocks, tile)
+    x0, x1 = xs[0], xs[1]
+    xcols = xs[2:]
+    n0, n1 = ns[0], ns[1]
 
     cols = my_col + n_col * jnp.arange(blocks, dtype=jnp.int32)
     rows = jnp.concatenate([my_row[None], cols])
-    xr_all = jnp.concatenate([points[None], xcols], axis=0).reshape(-1, points.shape[1])
     nr = len(rows)
+    xr_all = jnp.concatenate([points[None], xcols], axis=0).reshape(nr * tile, cov)
     eye = jnp.eye(tile, dtype=jnp.float32)
+    rmask = lambda m: m[:, None, None]
 
-    x01 = jnp.concatenate([x0, x1], axis=0)
-    k01 = kernel_tile(x01, x01, weights)
-    a00 = k01[:tile, :tile] + eye * n0[None, :]
-    a10 = k01[tile:, :tile]
-    a11 = k01[tile:, tile:] + eye * n1[None, :]
+    a00 = kernel_tile(x0, x0, weights) + eye * n0[None, :]
+    a10 = kernel_tile(x1, x0, weights)
+    a11 = kernel_tile(x1, x1, weights) + eye * n1[None, :]
 
-    kr = kernel_tile(xr_all, x01, weights).reshape(nr, tile, 2 * tile)
     bs = band_start[rows]
-    keep0 = (bs <= 0)[:, None, None]
-    keep1 = ((bs <= 1) & (rows >= 1))[:, None, None]
-    ar0 = jnp.where(keep0, kr[:, :, :tile], 0.0)
-    ar0 = ar0 + jnp.where((rows == 0)[:, None, None], eye * n0[None, :], 0.0)
-    ar1 = jnp.where(keep1, kr[:, :, tile:], 0.0)
-    ar1 = ar1 + jnp.where((rows == 1)[:, None, None], eye * n1[None, :], 0.0)
+    kr0 = kernel_tile(xr_all, x0, weights).reshape(nr, tile, tile)
+    ar0 = jnp.where(rmask(bs <= 0), kr0, 0.0) + jnp.where(rmask(rows == 0), eye * n0[None, :], 0.0)
+    kr1 = kernel_tile(xr_all, x1, weights).reshape(nr, tile, tile)
+    ar1 = jnp.where(rmask((bs <= 1) & (rows >= 1)), kr1, 0.0)
+    ar1 = ar1 + jnp.where(rmask(rows == 1), eye * n1[None, :], 0.0)
 
     l00, m0 = chol_inv(a00)
-    stack0 = jnp.concatenate([a10, ar0.reshape(-1, tile)], axis=0)
-    sol0 = mm(stack0, m0)
-    l01 = sol0[:tile]
-    lr0 = sol0[tile:].reshape(nr, tile, tile)
-    lr0 = jnp.where((rows == 0)[:, None, None], l00[None], lr0)
+    l01 = mm(a10, m0)
+    lr0 = mm(ar0.reshape(nr * tile, tile), m0).reshape(nr, tile, tile)
+    lr0 = jnp.where(rmask(rows == 0), l00[None], lr0)
 
-    s11 = a11 - mm(l01, l01)
-    upd1 = mm(lr0.reshape(-1, tile), l01).reshape(nr, tile, tile)
-    ar1 = ar1 - jnp.where((rows >= 1)[:, None, None], upd1, 0.0)
-    l11, m1 = chol_inv(s11)
-    lr1 = mm(ar1.reshape(-1, tile), m1).reshape(nr, tile, tile)
-    lr1 = jnp.where((rows > 1)[:, None, None], lr1, jnp.where((rows == 1)[:, None, None], l11[None], 0.0))
+    l11, m1 = chol_inv(a11 - mm(l01, l01))
+    upd1 = mm(lr0.reshape(nr * tile, tile), l01).reshape(nr, tile, tile)
+    ar1 = ar1 - jnp.where(rmask(rows >= 1), upd1, 0.0)
+    lr1 = mm(ar1.reshape(nr * tile, tile), m1).reshape(nr, tile, tile)
+    lr1 = jnp.where(rmask(rows > 1), lr1, jnp.where(rmask(rows == 1), l11[None], 0.0))
 
-    kout = kernel_tile(points, xcols.reshape(-1, points.shape[1]), weights)
-    kout = kout.reshape(tile, blocks, tile).transpose(1, 0, 2)
     bsr = band_start[my_row]
-    keep = ((cols >= bsr) & (cols <= my_row))[:, None, None]
-    aout = jnp.where(keep, kout, 0.0)
-    aout = aout + jnp.where((cols == my_row)[:, None, None], eye * nugget[None, :], 0.0)
-    left = jnp.concatenate([lr0[0], lr1[0]], axis=1)
-    right = jnp.concatenate([lr0[1:], lr1[1:]], axis=2).reshape(-1, 2 * tile)
-    prod = mm(left, right, lax.Precision.HIGH).reshape(tile, blocks, tile).transpose(1, 0, 2)
-    live = ((cols > 1) & (cols <= my_row))[:, None, None]
-    res = aout - jnp.where(live, prod, 0.0)
-    res = jnp.where((cols == 0)[:, None, None], lr0[0][None], res)
-    res = jnp.where((cols == 1)[:, None, None], lr1[0][None], res)
-    return res.reshape(1, blocks, 1, tile, tile)
+    out = []
+    for k in range(blocks):
+        col = cols[k]
+        a = kernel_tile(points, xcols[k], weights)
+        a = jnp.where((col >= bsr) & (col <= my_row), a, 0.0)
+        a = a + jnp.where(col == my_row, eye * nugget[None, :], 0.0)
+        prod = mm(lr0[0], lr0[1 + k], lax.Precision.HIGH) + mm(lr1[0], lr1[1 + k], lax.Precision.HIGH)
+        res = a - jnp.where((col > 1) & (col <= my_row), prod, 0.0)
+        res = jnp.where(col == 0, lr0[0], jnp.where(col == 1, lr1[0], res))
+        out.append(res)
+    return jnp.stack(out).reshape(1, blocks, 1, tile, tile)
 
 
 def solution(mesh):

time: 441 us -> 393 us (0.89)
  blocking collectives: 72.9 us -> 0 us
  waiting for transfers between devices: 16.7 us -> 74.6 us
  local copies, waits for them, and re-layouts: 66.2 us -> 33.9 us
  between operations: 14.6 us -> 32.5 us
  other arithmetic: 34 us -> 16.2 us
    psum x1 -> x0, blocking collectives: 72.9 us -> none  [body(): nug = lax.psum(jnp.where(slot, nugget[None, :], 0.0), 'row')]
    all_gather x1, waiting for transfers between devices: 0.01 us -> 57.7 us  [body(): got = lax.all_gather(sel, 'row', axis=1)]
    unnamed x101 -> x154, local copies, waits for them, and re-layouts: 22.5 us -> 6.86 us
    select_n x3 -> x0, other arithmetic: 9.64 us -> none  [the longest x2 8.89 us: body(): lr0 = jnp.where((rows == 0)[:, None, None], l00[None], lr0)]
    add x2 -> x0, other arithmetic: 7.28 us -> none  [the longest x1 5.93 us: body(): ar0 = ar0 + jnp.where((rows == 0)[:, None, None], eye * n0[None, :], 0.0)]
    broadcast_in_dim x6 -> x4, local copies, waits for them, and re-layouts: 7.94 us -> 1.36 us  [the longest x2 0.69 us: body(): jnp.where(rmask(bs <= 0), kr0, 0.0)]
    add x1 -> x0, local copies, waits for them, and re-layouts: 5.95 us -> none  [body(): ar0 = ar0 + jnp.where((rows == 0)[:, None, None], eye * n0[None, :], 0.0)]
    dot_general x20 -> x34, matrix products: 88.6 us -> 88.6 us  [mm(): lax.dot_general(a, b, (((1,), (1,)), ((), ())), precision=precision, pref...]
  transfers between devices with their start and end apart: 2 -> 2, of which waited for: 1 -> 2; matrix products, arithmetic and copies ran while one was open for 2% -> 1% of each run, Pallas kernels for 0% -> 0%
where the time goes in v6:
time: 393 us; the launch traced here: 386 us
  Pallas kernels  116 us (30%)
  matrix products  102 us (26%)
  waiting for transfers between devices  74.6 us (19%)
  local copies, waits for them, and re-layouts  33.9 us (9%)
  between operations  32.5 us (8%)
  other arithmetic  16.2 us (4%)
  starting transfers between devices  11.4 us (3%)
    pallas_call x8, Pallas kernels, chol_base(): pl.pallas_call(_chol_base_kernel, out_shape=(jax.ShapeDtypeStruct((n, n),...  116 us
    dot_general x34, matrix products, mm(): lax.dot_general(a, b, (((1,), (1,)), ((), ())), precision=precision, pref...  88.6 us
    all_gather x1, waiting for transfers between devices, body(): got = lax.all_gather(sel, 'row', axis=1)  57.7 us
    all_to_all x1, waiting for transfers between devices, body(): lax.all_to_all(jnp.concatenate([flat, nug_pad], axis=1), 'row', 0, 0, til...  16.9 us
    dot_general x12, matrix products, dot(): return jnp.dot(a, b, precision=HI, preferred_element_type=jnp.float32)  13 us
    all_to_all x1, starting transfers between devices, body(): lax.all_to_all(jnp.concatenate([flat, nug_pad], axis=1), 'row', 0, 0, til...  11.3 us
  transfers between devices with their start and end apart: 2, of which 2 were waited for; matrix products, arithmetic and copies ran while one was open for 1% of the time, Pallas kernels for 0%

profile of v6, /device:TPU:8, one launch (start us, length us, event | category | flops | bytes accessed | tf_op | source)
XLA Modules:
  0.0 386.4 jit_solution(15080899675725920577)
XLA Ops:
  9.7 11.3 %all-to-all-start = ((f32[32,1,4224]{2,1,0:T(1,128)}), f32[32,1,4224]{2,1,0:T(1,128)S(1)}, u32[]{:S(2)}, u32[]{:S(2)}) async-start(f32[32,1,4224]{2,1,0:T(1,128)} %all_to_all.6), calls=%async_computation | async-start | bytes 1081344 | tf_op jit(solution)/shard_map/all_to_all | solution.py:108
  21.1 16.9 %all-to-all-done = f32[32,1,4224]{2,1,0:T(1,128)S(1)} async-done(((f32[32,1,4224]{2,1,0:T(1,128)}), f32[32,1,4224]{2,1,0:T(1,128)S(1)}, u32[]{:S(2)}, u32[]{:S(2)}) %all-to-all-start) | async-done | bytes 540704 | tf_op jit(solution)/shard_map/all_to_all | solution.py:108
  60.8 57.7 %all-gather.3.cloned.1.call-done = f32[6,135168]{1,0:T(8,128)} async-done(((f32[6,4224]{1,0:T(8,128)}), f32[6,135168]{1,0:T(8,128)}) %all-gather.3.cloned.1.call-update) | async-done | bytes 3244048 | tf_op jit(solution)/shard_map/all_gather | solution.py:112
  118.6 2.9 copy.57
  128.8 2.1 mul.389
  131.0 2.3 multiply_reduce_fusion.5
  133.3 2.2 multiply_add_fusion
  137.1 14.6 %shard_map.46 = (f32[128,128]{1,0:T(8,128)}, f32[128,128]{1,0:T(8,128)}) custom-call(f32[128,128]{1,0:T(8,128)} %slice.214.a_ref), custom_call_target="tpu_custom_call" | custom-call | tf_op jit(solution)/shard_map/pallas_call | solution.py:68
  156.6 2.0 fusion.42
  158.6 2.0 fusion.38
  160.6 14.5 %shard_map.47 = (f32[128,128]{1,0:T(8,128)}, f32[128,128]{1,0:T(8,128)}) custom-call(f32[128,128]{1,0:T(8,128)} %convolution_subtract_fusion.6.a_ref), custom_call_target="tpu_custom_call" | custom-call | tf_op jit(solution)/shard_map/pallas_call | solution.py:68
  180.0 14.4 %shard_map.48 = (f32[128,128]{1,0:T(8,128)}, f32[128,128]{1,0:T(8,128)}) custom-call(f32[128,128]{1,0:T(8,128)} %slice.219.a_ref), custom_call_target="tpu_custom_call" | custom-call | tf_op jit(solution)/shard_map/pallas_call | solution.py:68
  196.4 14.4 %shard_map.49 = (f32[128,128]{1,0:T(8,128)}, f32[128,128]{1,0:T(8,128)}) custom-call(f32[128,128]{1,0:T(8,128)} %convolution_subtract_fusion.5.a_ref), custom_call_target="tpu_custom_call" | custom-call | tf_op jit(solution)/shard_map/pallas_call | solution.py:68
  218.8 2.8 fusion.89
  222.6 1.9 convolution_subtract_fusion
  225.2 14.4 %shard_map.50 = (f32[128,128]{1,0:T(8,128)}, f32[128,128]{1,0:T(8,128)}) custom-call(f32[128,128]{1,0:T(8,128)} %slice.226.a_ref), custom_call_target="tpu_custom_call" | custom-call | tf_op jit(solution)/shard_map/pallas_call | solution.py:68
  241.6 14.4 %shard_map.51 = (f32[128,128]{1,0:T(8,128)}, f32[128,128]{1,0:T(8,128)}) custom-call(f32[128,128]{1,0:T(8,128)} %convolution_subtract_fusion.4.a_ref), custom_call_target="tpu_custom_call" | custom-call | tf_op jit(solution)/shard_map/pallas_call | solution.py:68
  260.8 14.9 %shard_map.52 = (f32[128,128]{1,0:T(8,128)}, f32[128,128]{1,0:T(8,128)}) custom-call(f32[128,128]{1,0:T(8,128)} %slice.231.a_ref), custom_call_target="tpu_custom_call" | custom-call | tf_op jit(solution)/shard_map/pallas_call | solution.py:68
  289.4 2.0 multiply_reduce_fusion
  292.1 7.6 %exponential_multiply_fusion = f32[2560,512]{1,0:T(8,128)} fusion(f32[2560,256]{1,0:T(8,128)S(1)} %bitcast.173, f32[512,256]{1,0:T(8,128)} %squeeze.84, f32[512]{0:T(512)} %copy-done.62, f32[2560]{0:T(1024)} %add.245), kind=kOutput, calls=%fused_computation.10 | convolution fusion | flops 2023751680 | bytes 8400896 | tf_op jit(solution)/shard_map/dot_general | solution.py:12
  299.9 5.4 %fusion = f32[2560,512]{1,0:T(8,128)S(1)} fusion(f32[2560,256]{1,0:T(8,128)S(1)} %bitcast.174, f32[512,256]{1,0:T(8,128)S(1)} %copy-done.7, f32[512,512]{1,0:T(8,128)S(1)} %copy-done.15, f32[512]{0:T(512)S(1)} %copy-done.55, f32[2560]{0:T(1024)S(1)} %copy-done.52, pred[2560]{0:T(1024)(128)(4,1)S(1)} %copy-done.56, pred[2560]{0:T(1024)(128)(4,1)S(1)} %copy-done.57), kind=kOutput, calls=%fused_computation.2 | convolution fusion | flops 2027683840 | bytes 9454592 | tf_op jit(solution)/shard_map/dot_general | solution.py:12
  305.5 8.8 %broadcast_select_fusion = f32[5,512,512]{2,1,0:T(8,128)S(1)} fusion(f32[512,512]{1,0:T(8,128)S(1)} %fusion.77, pred[5]{0:T(512)(128)(4,1)S(1)} %copy-done.64, f32[5,512,512]{2,1,0:T(8,128)S(1)} %bitcast.172, f32[256,256]{1,0:T(8,128)S(1)} %copy-done.25, f32[128,128]{1,0:T(8,128)S(1)} %copy-done.34, f32[128,128]{1,0:T(8,128)S(1)} %copy-done.36, ...), kind=kOutput, calls=%fused_computation.17 | convolution fusion | flops 8055947264 | bytes 12320773 | tf_op jit(solution)/shard_map/dot_general | solution.py:12
  314.3 10.1 %fusion.86 = f32[5,512,512]{2,1,0:T(8,128)} fusion(f32[5,512,512]{2,1,0:T(8,128)S(1)} %broadcast_select_fusion, f32[512,512]{1,0:T(8,128)S(1)} %copy-done.5), kind=kOutput, calls=%fused_computation.138 | convolution fusion | flops 8053063680 | bytes 11534336 | tf_op jit(solution)/shard_map/dot_general | solution.py:12
  324.4 2.0 fusion.70
  326.4 2.0 fusion.69
  328.4 2.1 fusion.68
  330.5 2.0 fusion.67
  332.5 14.6 %shard_map.53 = (f32[128,128]{1,0:T(8,128)}, f32[128,128]{1,0:T(8,128)}) custom-call(f32[128,128]{1,0:T(8,128)} %convolution_subtract_fusion.3.a_ref), custom_call_target="tpu_custom_call" | custom-call | tf_op jit(solution)/shard_map/pallas_call | solution.py:68
  352.2 2.1 fusion.34
  354.3 1.8 fusion.29
  358.5 12.5 %select_select_fusion = f32[5,512,512]{2,1,0:T(8,128)S(1)} fusion(f32[5,512,512]{2,1,0:T(8,128)S(1)} %bitcast.176, f32[5,512,512]{2,1,0:T(8,128)} %bitcast.182, f32[512,512]{1,0:T(8,128)S(1)} %fusion.72, f32[512,512]{1,0:T(8,128)S(1)} %copy-done.29, pred[5]{0:T(512)(128)(4,1)S(1)} %copy-done.68, pred[5]{0:T(512)(128)(4,1)S(1)} %copy-done.67, ...), kind=kOutput, calls=%fused_computation.3 | convolution fusion | flops 8063811584 | bytes 18612244 | tf_op jit(solution)/shard_map/dot_general | solution.py:12
  376.7 2.5 maximum_bitcast_fusion
  (240 shorter events, 72.5 us)
Async XLA Ops:
  6.5 35.7 %copy-start = (s32[32]{0:T(128)S(1)}, s32[32]{0:T(128)}, u32[]{:S(2)}) copy-start(s32[32]{0:T(128)} %param.7) | copy-start | bytes 388
  6.5 51.0 %copy-start.50 = (f32[256]{0:T(256)S(1)}, f32[256]{0:T(256)}, u32[]{:S(2)}) copy-start(f32[256]{0:T(256)} %param.6) | copy-start | bytes 3076
  9.7 28.2 %all-to-all-start = ((f32[32,1,4224]{2,1,0:T(1,128)}), f32[32,1,4224]{2,1,0:T(1,128)S(1)}, u32[]{:S(2)}, u32[]{:S(2)}) async-start(f32[32,1,4224]{2,1,0:T(1,128)} %all_to_all.6), calls=%async_computation | async-start | bytes 1081344 | tf_op jit(solution)/shard_map/all_to_all | solution.py:108
  21.0 97.5 %all-gather.3.cloned.1.call-start = ((), (), s32[]{:S(2)}) async-start(), calls=%async_computation.1 | async-start | bytes 4460544 | tf_op jit(solution)/shard_map/all_gather | solution.py:112
  59.5 62.0 %copy-start.63 = (pred[5]{0:T(512)(128)(4,1)}, pred[5]{0:T(512)(128)(4,1)S(1)}, u32[]{:S(2)}) copy-start(pred[5]{0:T(512)(128)(4,1)S(1)} %get-tuple-element.69) | copy-start | bytes 19
  126.0 30.6 %copy-start.6 = (f32[512,256]{1,0:T(8,128)}, f32[512,256]{1,0:T(8,128)S(1)}, u32[]{:S(2)}) copy-start(f32[512,256]{1,0:T(8,128)S(1)} %squeeze.82) | copy-start | bytes 1572868
  127.1 49.1 %copy-start.14 = (f32[512,256]{1,0:T(8,128)}, f32[512,256]{1,0:T(8,128)S(1)}, u32[]{:S(2)}) copy-start(f32[512,256]{1,0:T(8,128)S(1)} %squeeze.87) | copy-start | bytes 1572868
  127.3 29.3 %copy-start.10 = (f32[512,256]{1,0:T(8,128)}, f32[512,256]{1,0:T(8,128)S(1)}, u32[]{:S(2)}) copy-start(f32[512,256]{1,0:T(8,128)S(1)} %squeeze.95) | copy-start | bytes 1572868
  128.8 26.7 %copy-start.8 = (f32[512,256]{1,0:T(8,128)}, f32[512,256]{1,0:T(8,128)S(1)}, u32[]{:S(2)}) copy-start(f32[512,256]{1,0:T(8,128)S(1)} %squeeze.99) | copy-start | bytes 1572868
  133.3 41.8 %copy-start.54 = (f32[512]{0:T(512)}, f32[512]{0:T(512)S(1)}, u32[]{:S(2)}) copy-start(f32[512]{0:T(512)S(1)} %get-tuple-element.46) | copy-start | bytes 6148
  133.3 41.8 %copy-start.62 = (f32[512]{0:T(512)}, f32[512]{0:T(512)S(1)}, u32[]{:S(2)}) copy-start(f32[512]{0:T(512)S(1)} %get-tuple-element.37) | copy-start | bytes 6148
  151.8 24.5 %copy-start.16 = (f32[128,128]{1,0:T(8,128)S(1)}, f32[128,128]{1,0:T(8,128)}, u32[]{:S(2)}) copy-start(f32[128,128]{1,0:T(8,128)} %get-tuple-element.22) | copy-start | bytes 196612
  160.6 58.2 %copy-start.30 = (f32[512,512]{1,0:T(8,128)S(1)}, f32[512,512]{1,0:T(8,128)}, u32[]{:S(2)}) copy-start(f32[512,512]{1,0:T(8,128)} %fusion.42) | copy-start | bytes 3145732
  213.0 11.5 %copy-start.35 = (f32[128,128]{1,0:T(8,128)}, f32[128,128]{1,0:T(8,128)S(1)}, u32[]{:S(2)}) copy-start(f32[128,128]{1,0:T(8,128)S(1)} %convolution_negate_fusion.4) | copy-start | bytes 196612
  216.4 25.2 %copy-start.31 = (f32[256,256]{1,0:T(8,128)}, f32[256,256]{1,0:T(8,128)S(1)}, u32[]{:S(2)}) copy-start(f32[256,256]{1,0:T(8,128)S(1)} %convolution_negate_fusion.1) | copy-start | bytes 786436
  224.6 60.2 %copy-start.59 = (f32[512]{0:T(512)S(1)}, f32[512]{0:T(512)}, u32[]{:S(2)}) copy-start(f32[512]{0:T(512)} %copy-done.58) | copy-start | bytes 6148
  258.2 29.7 %copy-start.33 = (f32[128,128]{1,0:T(8,128)}, f32[128,128]{1,0:T(8,128)S(1)}, u32[]{:S(2)}) copy-start(f32[128,128]{1,0:T(8,128)S(1)} %convolution_negate_fusion.3) | copy-start | bytes 196612
  314.3 16.2 %copy-start.1 = (f32[5,512,512]{2,1,0:T(8,128)}, f32[5,512,512]{2,1,0:T(8,128)S(1)}, u32[]{:S(2)}) copy-start(f32[5,512,512]{2,1,0:T(8,128)S(1)} %broadcast_select_fusion) | copy-start | bytes 15728644
  326.4 24.4 %copy-start.17 = (f32[128,128]{1,0:T(8,128)S(1)}, f32[128,128]{1,0:T(8,128)}, u32[]{:S(2)}) copy-start(f32[128,128]{1,0:T(8,128)} %get-tuple-element.29) | copy-start | bytes 196612
  326.4 25.7 %copy-start.49 = (f32[512]{0:T(512)S(1)}, f32[512]{0:T(512)}, u32[]{:S(2)}) copy-start(f32[512]{0:T(512)} %get-tuple-element.44) | copy-start | bytes 6148
  326.4 25.7 %copy-start.51 = (f32[256]{0:T(256)S(1)}, f32[256]{0:T(256)}, u32[]{:S(2)}) copy-start(f32[256]{0:T(256)} %param.6) | copy-start | bytes 3076
  328.4 25.9 %copy-start.13 = (f32[512,256]{1,0:T(8,128)S(1)}, f32[512,256]{1,0:T(8,128)}, u32[]{:S(2)}) copy-start(f32[512,256]{1,0:T(8,128)} %copy-done.12) | copy-start | bytes 1572868
  330.5 25.6 %copy-start.11 = (f32[512,256]{1,0:T(8,128)S(1)}, f32[512,256]{1,0:T(8,128)}, u32[]{:S(2)}) copy-start(f32[512,256]{1,0:T(8,128)} %copy-done.10) | copy-start | bytes 1572868
  330.5 25.6 %copy-start.61 = (f32[512]{0:T(512)S(1)}, f32[512]{0:T(512)}, u32[]{:S(2)}) copy-start(f32[512]{0:T(512)} %get-tuple-element.43) | copy-start | bytes 6148
  330.5 26.6 %copy-start.9 = (f32[512,256]{1,0:T(8,128)S(1)}, f32[512,256]{1,0:T(8,128)}, u32[]{:S(2)}) copy-start(f32[512,256]{1,0:T(8,128)} %copy-done.8) | copy-start | bytes 1572868
  330.5 26.6 %copy-start.60 = (f32[512]{0:T(512)S(1)}, f32[512]{0:T(512)}, u32[]{:S(2)}) copy-start(f32[512]{0:T(512)} %get-tuple-element.45) | copy-start | bytes 6148
  330.5 27.8 %slice-start.2 = ((s8[5242880]{0:T(1024)(128)(4,1)}), s8[1048576]{0:T(1024)(128)(4,1)S(1)}, s32[]{:S(2)}) async-start(s8[5242880]{0:T(1024)(128)(4,1)} %bitcast.175), calls=%async_computation.4 | async-start | bytes 2097152
  347.2 11.0 %copy-start.48 = (f32[128,128]{1,0:T(8,128)S(1)}, f32[128,128]{1,0:T(8,128)}, u32[]{:S(2)}) copy-start(f32[128,128]{1,0:T(8,128)} %get-tuple-element.34) | copy-start | bytes 196612
  358.2 12.8 %slice-start = ((s8[5242880]{0:T(1024)(128)(4,1)}), s8[4194304]{0:T(1024)(128)(4,1)S(1)}, s32[]{:S(2)}) async-start(s8[5242880]{0:T(1024)(128)(4,1)} %bitcast.166), calls=%async_computation.2 | async-start | bytes 8388608
  358.4 12.6 %slice-start.1 = ((s8[5242880]{0:T(1024)(128)(4,1)}), s8[1048576]{0:T(1024)(128)(4,1)S(1)}, s32[]{:S(2)}) async-start(s8[5242880]{0:T(1024)(128)(4,1)} %bitcast.166), calls=%async_computation.3 | async-start | bytes 2097152
  358.5 12.6 %copy-start.23 = (f32[512,512]{1,0:T(8,128)S(1)}, f32[512,512]{1,0:T(8,128)}, u32[]{:S(2)}) copy-start(f32[512,512]{1,0:T(8,128)} %fusion.70) | copy-start | bytes 3145732
  358.5 12.6 %copy-start.65 = (f32[512]{0:T(512)S(1)}, f32[512]{0:T(512)}, u32[]{:S(2)}) copy-start(f32[512]{0:T(512)} %param.5) | copy-start | bytes 6148
  (44 other events, 275.2 us)
Sparse Core Ops, SparseCore 0:
  38.9 79.5 all-gather.2
